TPU v7x, 128 devices: a whole 4x4x4 slice. The times are simulated.
128 devices in a mesh: blk: 8 (over y, x_hi), terms: 16 (over z, x_lo, core).
Axes of the slice: x: 4 (x_hi: 2, x_lo: 2; x = x_hi * 2 + x_lo), y: 4, z: 4, core: 2. Of those that a mesh axis runs over, the one named last changes fastest.
Arguments:
- wavefunction: bfloat16 [16, 256, 256], P('blk'), may hold values from -6 to 6
- left_terms: bfloat16 [8192, 256, 256], P(('blk', 'terms')), may hold values from -0.375 to 0.375
- right_terms: bfloat16 [8192, 256, 256], P(('blk', 'terms')), may hold values from -0.015625 to 0.015625
- term_slab: int32 [8192, 1], P(('blk', 'terms')), may hold values from 0 to 7; in each aligned block of 64 rows (0 to 63, 64 to 127, ...) at most 32 rows name the same one
- term_sector: int32 [8192], P(('blk', 'terms')), may hold values from 0 to 1
- term_target: int32 [8192], P(('blk', 'terms')), may hold values from 0 to 15
Outputs:
- sigma: float32 [4096, 256], P(('blk', 'terms'))
Inputs may be any that keep to these rules, and one draw needn't show every extreme that they name: `term_slab`: of the 64 terms of one device at most 32 name the same slab.
All inputs are finite; a program needn't handle non-finite values.
Results may differ from a plain program's by a relative error of at most 0.0029.
Values may be sent and summed in bfloat16 or wider, within the bound.
No kernel may reach another device: no remote copies, remote signals or barrier semaphores. Data moves between devices by JAX's collectives and lax.ppermute only.
A program may use at most 256 MiB of HBM per device.

v0:
```python
import jax
import jax.numpy as jnp
from jax import lax
from jax.sharding import PartitionSpec as P


def add_terms(running, wave_blocks, left_block, right_block, local_rows, targets):
    psi_blocks = wave_blocks[local_rows]
    left_part = jnp.einsum(
        "tij,tjk->tik", left_block, psi_blocks, preferred_element_type=jnp.float32
    ).astype(jnp.bfloat16)
    term_image = jnp.einsum(
        "tik,tlk->til", left_part, right_block, preferred_element_type=jnp.float32
    )
    return running.at[targets].add(term_image)


def on_device(wavefunction, left_terms, right_terms, term_slab, term_sector, term_target):
    per_slab = wavefunction.shape[0]
    cycle_size = lax.axis_size("blk")
    sectors = per_slab * cycle_size
    block_width = wavefunction.shape[1]
    slab_index = term_slab[:, 0]
    partial_value = jnp.zeros((sectors, block_width, block_width), jnp.float32)
    gathered = lax.all_gather(wavefunction, "blk", axis=0, tiled=True)
    partial_value = add_terms(
        partial_value,
        gathered,
        left_terms,
        right_terms,
        slab_index * per_slab + term_sector,
        term_target,
    )
    stacked = partial_value.reshape(sectors * block_width, block_width)
    return lax.psum_scatter(stacked, ("blk", "terms"), scatter_dimension=0, tiled=True)


def solution(mesh):
    placed = (
        P("blk", None, None),
        P(("blk", "terms"), None, None),
        P(("blk", "terms"), None, None),
        P(("blk", "terms"), None),
        P(("blk", "terms")),
        P(("blk", "terms")),
    )
    return jax.shard_map(
        on_device, mesh=mesh, in_specs=placed, out_specs=P(("blk", "terms"), None), check_vma=False
    )
```

profile of v0, /device:TPU:0, one launch (start us, length us, event | category | flops | bytes accessed | tf_op | source)
XLA Modules:
  0.0 782.6 jit_solution(494243670613129015)
XLA Ops:
  6.5 0.0 all-gather.2.cloned.1.call-start
  6.5 0.7 all-gather.2.cloned.1.call-update
  7.3 0.0 reduce-scatter.2.cloned.1.call-start
  7.3 0.7 compare_select_fusion
  8.0 0.7 compare_select_fusion.1
  8.6 57.0 %all-gather.2.cloned.1.call-done = bf16[16,256,256]{2,1,0:T(8,128)(2,1)} async-done(((bf16[2,256,256]{2,1,0:T(8,128)(2,1)}), bf16[16,256,256]{2,1,0:T(8,128)(2,1)}) %all-gather.2.cloned.1.call-update) | async-done | bytes 2097168 | tf_op jit(solution)/shard_map/all_gather | solution.py:25
  65.6 7.1 gather_fusion
  72.7 16.7 %fusion = f32[64,256,256]{2,1,0:T(8,128)} fusion(bf16[64,256,256]{2,1,0:T(8,128)(2,1)} %param.8, bf16[64,256,256]{2,1,0:T(8,128)(2,1)} %param.7, bf16[64,256,256]{2,1,0:T(8,128)(2,1)} %gather_fusion), kind=kOutput, calls=%fused_computation.2 | convolution fusion | flops 4299161600 | bytes 41943040 | tf_op jit(solution)/shard_map/tik,tlk->til/dot_general | solution.py:12
  89.4 2.4 broadcast_in_dim.9
  91.7 36.6 %scatter_fusion = f32[16,256,256]{2,1,0:T(8,128)} fusion(f32[16,256,256]{2,1,0:T(8,128)} %broadcast_in_dim.9, s32[64]{0:T(128)S(1)} %compare_select_fusion.1, f32[64,256,256]{2,1,0:T(8,128)} %fusion), kind=kCustom, calls=%fused_computation.1 | custom fusion | flops 4194304 | bytes 50331904 | tf_op jit(solution)/shard_map/scatter-add | solution.py:15
  128.3 0.0 reduce-scatter.2.cloned.1.call-update
  128.4 647.4 %reduce-scatter.2.cloned.1.call-done = f32[32,256]{1,0:T(8,128)} async-done(((f32[4096,256]{1,0:T(8,128)}), f32[32,256]{1,0:T(8,128)}) %reduce-scatter.2.cloned.1.call-update) | async-done | bytes 32784 | tf_op jit(solution)/shard_map/reduce_scatter | solution.py:35
  (1 shorter events, 0.0 us)
Async XLA Ops:
  6.5 59.1 %all-gather.2.cloned.1.call-start = ((), (), s32[]{:S(2)}) async-start(), calls=%async_computation.1 | async-start | bytes 2359296 | tf_op jit(solution)/shard_map/all_gather | solution.py:25
  7.3 768.5 %reduce-scatter.2.cloned.1.call-start = ((), (), s32[]{:S(2)}) async-start(), calls=%async_computation.2 | async-start | bytes 4227072 | tf_op jit(solution)/shard_map/reduce_scatter | solution.py:35
Sparse Core Ops, SparseCore 0:
  9.7 55.8 all-gather.1
  128.5 647.2 reduce-scatter.1
where the time goes:
time: 783 us
  waiting for transfers between devices  705 us (90%)
  other arithmetic  38 us (5%)
  matrix products  16.7 us (2%)
  between operations  13.4 us (2%)
  local copies, waits for them, and re-layouts  9.46 us (1%)
    reduce_scatter x1, waiting for transfers between devices, on_device(): lax.psum_scatter(stacked, ('blk', 'terms'), scatter_dimension=0, tiled=True)  647 us
    all_gather x1, waiting for transfers between devices, on_device(): gathered = lax.all_gather(wavefunction, 'blk', axis=0, tiled=True)  57 us
    scatter-add x1, other arithmetic, add_terms(): return running.at[targets].add(term_image)  36.6 us
    dot_general x1, matrix products, add_terms(): jnp.einsum('tik,tlk->til', left_part, right_block, preferred_element_type...  16.7 us
  transfers between devices with their start and end apart: 2, of which 2 were waited for; matrix products, arithmetic and copies ran while one was open for 0% of the time, Pallas kernels for 0%

commit v1 on v0

v1 whole, which is shorter than its diff:
```python
import jax
import jax.numpy as jnp
from jax import lax
from jax.sharding import Mesh
from jax.sharding import PartitionSpec as P

PHYS = ("y", "xh", "z", "xl", "c")


def add_terms(running, wave_blocks, left_block, right_block, local_rows, targets):
    psi_blocks = wave_blocks[local_rows]
    left_part = jnp.einsum(
        "tij,tjk->tik", left_block, psi_blocks, preferred_element_type=jnp.float32
    ).astype(jnp.bfloat16)
    term_image = jnp.einsum(
        "tik,tlk->til", left_part, right_block, preferred_element_type=jnp.float32
    )
    return running.at[targets].add(term_image)


def gather_blocks(wavefunction, n_blk):
    copies = jnp.broadcast_to(wavefunction[None], (n_blk,) + wavefunction.shape)
    got = lax.all_to_all(copies, ("y", "xh"), 0, 0, tiled=True)
    return got.reshape((-1,) + wavefunction.shape[1:])


def reduce_rows(stacked, n_core, n_rest):
    rows = stacked.shape[0] // (n_core * n_rest)
    y = stacked.reshape(n_rest, n_core, rows, stacked.shape[1]).transpose(1, 0, 2, 3)
    y = lax.all_to_all(y, "c", 0, 0, tiled=True).reshape(n_core, n_rest, rows, -1).sum(0)
    y = lax.all_to_all(y, ("y", "xh", "z", "xl"), 0, 0, tiled=True)
    return y.reshape(n_rest, rows, -1).sum(0)


def on_device(wavefunction, left_terms, right_terms, term_slab, term_sector, term_target):
    per_slab = wavefunction.shape[0]
    n_blk = lax.axis_size(("y", "xh"))
    n_core = lax.axis_size("c")
    n_rest = lax.axis_size(("y", "xh", "z", "xl"))
    sectors = per_slab * n_blk
    block_width = wavefunction.shape[1]
    slab_index = term_slab[:, 0]
    partial_value = jnp.zeros((sectors, block_width, block_width), jnp.float32)
    gathered = gather_blocks(wavefunction, n_blk)
    partial_value = add_terms(
        partial_value,
        gathered,
        left_terms,
        right_terms,
        slab_index * per_slab + term_sector,
        term_target,
    )
    stacked = partial_value.reshape(sectors * block_width, block_width)
    return reduce_rows(stacked, n_core, n_rest)


def solution(mesh):
    blk, terms = mesh.axis_names
    n_blk, n_terms = mesh.shape[blk], mesh.shape[terms]
    n_core = 2
    phys = Mesh(
        mesh.devices.reshape(n_blk // 2, 2, n_terms // (2 * n_core), 2, n_core), PHYS
    )
    wave = ("y", "xh")
    spread = PHYS
    placed = (
        P(wave, None, None),
        P(spread, None, None),
        P(spread, None, None),
        P(spread, None),
        P(spread),
        P(spread),
    )
    return jax.shard_map(
        on_device, mesh=phys, in_specs=placed, out_specs=P(spread, None), check_vma=False
    )
```

time: 783 us -> 152 us (0.19)
  waiting for transfers between devices: 705 us -> 27.1 us
  blocking collectives: 0 us -> 45.3 us
  between operations: 13.4 us -> 0.02 us
    reduce_scatter x1 -> x0, waiting for transfers between devices: 647 us -> none  [on_device(): lax.psum_scatter(stacked, ('blk', 'terms'), scatter_dimension=0, tiled=True)]
    all_gather x1 -> x0, waiting for transfers between devices: 57 us -> none  [on_device(): gathered = lax.all_gather(wavefunction, 'blk', axis=0, tiled=True)]
    all_to_all x0 -> x2, blocking collectives: none -> 45.3 us  [the longest x1 37.1 us: reduce_rows(): y = lax.all_to_all(y, ('y', 'xh', 'z', 'xl'), 0, 0, tiled=True)]
    all_to_all x0 -> x1, waiting for transfers between devices: none -> 27.1 us  [gather_blocks(): got = lax.all_to_all(copies, ('y', 'xh'), 0, 0, tiled=True)]
  transfers between devices with their start and end apart: 2 -> 1, of which waited for: 2 -> 1; matrix products, arithmetic and copies ran while one was open for 0% -> 1% of each run, Pallas kernels for 0% -> 0%
where the time goes in v1:
time: 152 us
  blocking collectives  45.3 us (30%)
  other arithmetic  42.6 us (28%)
  waiting for transfers between devices  27.1 us (18%)
  matrix products  16.8 us (11%)
  local copies, waits for them, and re-layouts  12.9 us (8%)
  starting transfers between devices  7.04 us (5%)
    all_to_all x1, blocking collectives, reduce_rows(): y = lax.all_to_all(y, ('y', 'xh', 'z', 'xl'), 0, 0, tiled=True)  37.1 us
    scatter-add x1, other arithmetic, add_terms(): return running.at[targets].add(term_image)  36.1 us
    all_to_all x1, waiting for transfers between devices, gather_blocks(): got = lax.all_to_all(copies, ('y', 'xh'), 0, 0, tiled=True)  27.1 us
    dot_general x1, matrix products, add_terms(): jnp.einsum('tik,tlk->til', left_part, right_block, preferred_element_type...  16.8 us
    all_to_all x1, blocking collectives, reduce_rows(): lax.all_to_all(y, 'c', 0, 0, tiled=True).reshape(n_core, n_rest, rows, -1)  8.17 us
    all_to_all x1, starting transfers between devices, gather_blocks(): got = lax.all_to_all(copies, ('y', 'xh'), 0, 0, tiled=True)  7.04 us
    gather x1, local copies, waits for them, and re-layouts, add_terms(): psi_blocks = wave_blocks[local_rows]  5.49 us
  transfers between devices with their start and end apart: 1, of which 1 were waited for; matrix products, arithmetic and copies ran while one was open for 1% of the time, Pallas kernels for 0%

profile of v1, /device:TPU:0, one launch (start us, length us, event | category | flops | bytes accessed | tf_op | source)
XLA Modules:
  0.0 151.7 jit_solution(13071188206067081687)
XLA Ops:
  0.0 2.5 %broadcast_in_dim.17 = bf16[8,2,256,256]{3,2,1,0:T(8,128)(2,1)} broadcast(bf16[2,256,256]{2,1,0:T(8,128)(2,1)} %param.6), dimensions={1,2,3} | broadcast | bytes 2359296 | tf_op jit(solution)/shard_map/broadcast_in_dim | solution.py:22
  2.5 7.0 %all-to-all-start = ((bf16[8,2,256,256]{3,2,1,0:T(8,128)(2,1)}), bf16[8,2,256,256]{3,2,1,0:T(8,128)(2,1)S(1)}, u32[]{:S(2)}, u32[]{:S(2)}) async-start(bf16[8,2,256,256]{3,2,1,0:T(8,128)(2,1)} %broadcast_in_dim.17), calls=%async_computation | async-start | bytes 4194304 | tf_op jit(solution)/shard_map/all_to_all | solution.py:23
  9.5 0.7 compare_select_fusion
  10.2 0.7 compare_select_fusion.1
  10.9 27.1 %all-to-all-done = bf16[8,2,256,256]{3,2,1,0:T(8,128)(2,1)S(1)} async-done(((bf16[8,2,256,256]{3,2,1,0:T(8,128)(2,1)}), bf16[8,2,256,256]{3,2,1,0:T(8,128)(2,1)S(1)}, u32[]{:S(2)}, u32[]{:S(2)}) %all-to-all-start) | async-done | bytes 2097184 | tf_op jit(solution)/shard_map/all_to_all | solution.py:23
  38.0 5.5 %gather_fusion = bf16[64,256,256]{2,1,0:T(8,128)(2,1)} fusion(bf16[16,256,256]{2,1,0:T(8,128)(2,1)S(1)} %bitcast.12, s32[1024]{0:T(1024)S(1)} %pad_clamp_fusion), kind=kCustom, calls=%fused_computation | custom fusion | bytes 16777472 | tf_op jit(solution)/shard_map/gather | solution.py:11
  43.5 16.8 %fusion = f32[64,256,256]{2,1,0:T(8,128)} fusion(bf16[64,256,256]{2,1,0:T(8,128)(2,1)} %param.8, bf16[64,256,256]{2,1,0:T(8,128)(2,1)} %gather_fusion, bf16[64,256,256]{2,1,0:T(8,128)(2,1)} %param.7), kind=kOutput, calls=%fused_computation.2 | convolution fusion | flops 4299161600 | bytes 41943040 | tf_op jit(solution)/shard_map/tik,tlk->til/dot_general | solution.py:15
  60.3 2.4 %broadcast_in_dim.15 = f32[16,256,256]{2,1,0:T(8,128)} broadcast(f32[]{:T(128)} %constant.4.clone.1), dimensions={} | broadcast | bytes 4194308 | tf_op jit(solution)/shard_map/broadcast_in_dim | solution.py:43
  62.6 36.1 %scatter_fusion = f32[16,256,256]{2,1,0:T(8,128)} fusion(f32[16,256,256]{2,1,0:T(8,128)} %broadcast_in_dim.15, s32[64]{0:T(128)S(1)} %compare_select_fusion.1, f32[64,256,256]{2,1,0:T(8,128)} %fusion), kind=kCustom, calls=%fused_computation.1 | custom fusion | flops 4194304 | bytes 50331904 | tf_op jit(solution)/shard_map/scatter-add | solution.py:18
  98.7 2.5 %copy.14 = f32[2,64,32,256]{3,2,1,0:T(8,128)S(1)} copy(f32[2,64,32,256]{3,2,0,1:T(8,128)} %bitcast.11) | data formatting | bytes 8388608 | tf_op jit(solution)/shard_map/transpose | solution.py:29
  101.2 8.2 %all_to_all.15 = f32[2,64,32,256]{3,2,1,0:T(8,128)} all-to-all(f32[2,64,32,256]{3,2,1,0:T(8,128)S(1)} %copy.14), channel_id=1, replica_groups=mesh['y'=4,'xh'=2,'z'=4,'xl'=2,'c'=2] {'c'}, dimensions={0} | all-to-all | bytes 8388608 | tf_op jit(solution)/shard_map/all_to_all | solution.py:30
  109.4 2.8 %reduce_sum.18 = f32[64,32,256]{2,1,0:T(8,128)S(1)} reduce(f32[2,64,32,256]{3,2,1,0:T(8,128)} %all_to_all.15, f32[]{:T(128)} %constant.4.clone.1), dimensions={0}, to_apply=%region_1.0 | reduce | flops 524288 | bytes 6291460 | tf_op jit(solution)/shard_map/reduce_sum | solution.py:30
  112.2 37.1 %all_to_all.16 = f32[64,32,256]{2,1,0:T(8,128)} all-to-all(f32[64,32,256]{2,1,0:T(8,128)S(1)} %reduce_sum.18), channel_id=1, replica_groups=mesh['y'=4,'xh'=2,'z'=4,'xl'=2,'c'=2] {'y','xh','z','xl'}, dimensions={0} | all-to-all | bytes 4194304 | tf_op jit(solution)/shard_map/all_to_all | solution.py:31
  149.3 2.3 %reduce_sum.19 = f32[32,256]{1,0:T(8,128)} reduce(f32[64,32,256]{2,1,0:T(8,128)} %all_to_all.16, f32[]{:T(128)} %constant.4.clone.1), dimensions={0}, to_apply=%region_2.0 | reduce | flops 516096 | bytes 2129924 | tf_op jit(solution)/shard_map/reduce_sum | solution.py:32
  (1 shorter events, 0.0 us)
Async XLA Ops:
  2.5 35.5 %all-to-all-start = ((bf16[8,2,256,256]{3,2,1,0:T(8,128)(2,1)}), bf16[8,2,256,256]{3,2,1,0:T(8,128)(2,1)S(1)}, u32[]{:S(2)}, u32[]{:S(2)}) async-start(bf16[8,2,256,256]{3,2,1,0:T(8,128)(2,1)} %broadcast_in_dim.17), calls=%async_computation | async-start | bytes 4194304 | tf_op jit(solution)/shard_map/all_to_all | solution.py:23

commit v2 on v1

--- a/solution.py
+++ b/solution.py
@@ -1,21 +1,50 @@
 import jax
 import jax.numpy as jnp
 from jax import lax
+from jax.experimental import pallas as pl
+from jax.experimental.pallas import tpu as pltpu
 from jax.sharding import Mesh
 from jax.sharding import PartitionSpec as P
 
 PHYS = ("y", "xh", "z", "xl", "c")
+TERM_BLOCK = 8
 
 
-def add_terms(running, wave_blocks, left_block, right_block, local_rows, targets):
-    psi_blocks = wave_blocks[local_rows]
-    left_part = jnp.einsum(
-        "tij,tjk->tik", left_block, psi_blocks, preferred_element_type=jnp.float32
-    ).astype(jnp.bfloat16)
-    term_image = jnp.einsum(
-        "tik,tlk->til", left_part, right_block, preferred_element_type=jnp.float32
-    )
-    return running.at[targets].add(term_image)
+def sigma_kernel(src_ref, tgt_ref, psi_ref, left_ref, right_ref, out_ref):
+    step = pl.program_id(0)
+
+    @pl.when(step == 0)
+    def _():
+        out_ref[...] = jnp.zeros_like(out_ref)
+
+    for j in range(TERM_BLOCK):
+        t = step * TERM_BLOCK + j
+        left_part = jnp.dot(
+            left_ref[j], psi_ref[src_ref[t]], preferred_element_type=jnp.float32
+        ).astype(jnp.bfloat16)
+        term_image = lax.dot_general(
+            left_part, right_ref[j], (((1,), (1,)), ((), ())),
+            preferred_element_type=jnp.float32,
+        )
+        out_ref[tgt_ref[t]] += term_image
+
+
+def add_terms(wave_blocks, left_terms, right_terms, sources, targets):
+    sectors, width, _ = wave_blocks.shape
+    n_terms = left_terms.shape[0]
+    whole = pl.BlockSpec((sectors, width, width), lambda i, s, g: (0, 0, 0))
+    per_step = pl.BlockSpec((TERM_BLOCK, width, width), lambda i, s, g: (i, 0, 0))
+    return pl.pallas_call(
+        sigma_kernel,
+        out_shape=jax.ShapeDtypeStruct((sectors, width, width), jnp.float32),
+        grid_spec=pltpu.PrefetchScalarGridSpec(
+            num_scalar_prefetch=2,
+            grid=(n_terms // TERM_BLOCK,),
+            in_specs=[whole, per_step, per_step],
+            out_specs=whole,
+        ),
+        compiler_params=pltpu.CompilerParams(dimension_semantics=("arbitrary",)),
+    )(sources, targets, wave_blocks, left_terms, right_terms)
 
 
 def gather_blocks(wavefunction, n_blk):
@@ -39,17 +68,9 @@
     n_rest = lax.axis_size(("y", "xh", "z", "xl"))
     sectors = per_slab * n_blk
     block_width = wavefunction.shape[1]
-    slab_index = term_slab[:, 0]
-    partial_value = jnp.zeros((sectors, block_width, block_width), jnp.float32)
+    sources = term_slab[:, 0] * per_slab + term_sector
     gathered = gather_blocks(wavefunction, n_blk)
-    partial_value = add_terms(
-        partial_value,
-        gathered,
-        left_terms,
-        right_terms,
-        slab_index * per_slab + term_sector,
-        term_target,
-    )
+    partial_value = add_terms(gathered, left_terms, right_terms, sources, term_target)
     stacked = partial_value.reshape(sectors * block_width, block_width)
     return reduce_rows(stacked, n_core, n_rest)
 

time: 152 us -> 107 us (0.70)
  other arithmetic: 42.6 us -> 5.65 us
  matrix products: 16.8 us -> 0 us
  Pallas kernels: 0 us -> 14.3 us
  local copies, waits for them, and re-layouts: 12.9 us -> 6.37 us
    scatter-add x1 -> x0, other arithmetic: 36.1 us -> none  [add_terms(): return running.at[targets].add(term_image)]
    dot_general x1 -> x0, matrix products: 16.8 us -> none  [add_terms(): jnp.einsum('tik,tlk->til', left_part, right_block, preferred_element_type...]
    pallas_call x0 -> x1, Pallas kernels: none -> 14.3 us  [add_terms(): pl.pallas_call(sigma_kernel, out_shape=jax.ShapeDtypeStruct((sectors, wid...]
    gather x1 -> x0, local copies, waits for them, and re-layouts: 5.49 us -> none  [add_terms(): psi_blocks = wave_blocks[local_rows]]
    another operation x0 -> x1, local copies, waits for them, and re-layouts: none -> 2.5 us  [reduce_rows(): stacked.reshape(n_rest, n_core, rows, stacked.shape[1])]
    transpose x1 -> x0, local copies, waits for them, and re-layouts: 2.5 us -> none  [reduce_rows(): stacked.reshape(n_rest, n_core, rows, stacked.shape[1])]
    broadcast_in_dim x1 -> x0, local copies, waits for them, and re-layouts: 2.36 us -> none  [on_device(): partial_value = jnp.zeros((sectors, block_width, block_width), jnp.float32)]
  transfers between devices with their start and end apart: 1 -> 1, of which waited for: 1 -> 1; matrix products, arithmetic and copies ran while one was open for 1% -> 0% of each run, Pallas kernels for 0% -> 0%
where the time goes in v2:
time: 107 us
  blocking collectives  45.3 us (42%)
  waiting for transfers between devices  27.9 us (26%)
  Pallas kernels  14.3 us (13%)
  starting transfers between devices  7.04 us (7%)
  local copies, waits for them, and re-layouts  6.37 us (6%)
  other arithmetic  5.65 us (5%)
    all_to_all x1, blocking collectives, reduce_rows(): y = lax.all_to_all(y, ('y', 'xh', 'z', 'xl'), 0, 0, tiled=True)  37.1 us
    all_to_all x1, waiting for transfers between devices, gather_blocks(): got = lax.all_to_all(copies, ('y', 'xh'), 0, 0, tiled=True)  27.9 us
    pallas_call x1, Pallas kernels, add_terms(): pl.pallas_call(sigma_kernel, out_shape=jax.ShapeDtypeStruct((sectors, wid...  14.3 us
    all_to_all x1, blocking collectives, reduce_rows(): lax.all_to_all(y, 'c', 0, 0, tiled=True).reshape(n_core, n_rest, rows, -1)  8.17 us
    all_to_all x1, starting transfers between devices, gather_blocks(): got = lax.all_to_all(copies, ('y', 'xh'), 0, 0, tiled=True)  7.04 us
    reduce_sum x1, other arithmetic, reduce_rows(): lax.all_to_all(y, 'c', 0, 0, tiled=True).reshape(n_core, n_rest, rows, -1)  2.79 us
    broadcast_in_dim x1, local copies, waits for them, and re-layouts, gather_blocks(): copies = jnp.broadcast_to(wavefunction[None], (n_blk,) + wavefunction.shape)  2.53 us
    another operation x1, local copies, waits for them, and re-layouts, reduce_rows(): stacked.reshape(n_rest, n_core, rows, stacked.shape[1])  2.5 us
  transfers between devices with their start and end apart: 1, of which 1 were waited for; matrix products, arithmetic and copies ran while one was open for 0% of the time, Pallas kernels for 0%

profile of v2, /device:TPU:0, one launch (start us, length us, event | category | flops | bytes accessed | tf_op | source)
XLA Modules:
  0.0 106.6 jit_solution(6026642121066500119)
XLA Ops:
  0.0 0.0 copy-start.1
  0.0 0.0 copy-start.2
  0.0 2.5 %broadcast_in_dim.2 = bf16[8,2,256,256]{3,2,1,0:T(8,128)(2,1)} broadcast(bf16[2,256,256]{2,1,0:T(8,128)(2,1)} %param.6), dimensions={1,2,3} | broadcast | bytes 2359296 | tf_op jit(solution)/shard_map/broadcast_in_dim | solution.py:51
  2.5 7.0 %all-to-all-start = ((bf16[8,2,256,256]{3,2,1,0:T(8,128)(2,1)}), bf16[8,2,256,256]{3,2,1,0:T(8,128)(2,1)S(1)}, u32[]{:S(2)}, u32[]{:S(2)}) async-start(bf16[8,2,256,256]{3,2,1,0:T(8,128)(2,1)} %broadcast_in_dim.2), calls=%async_computation | async-start | bytes 4194304 | tf_op jit(solution)/shard_map/all_to_all | solution.py:52
  9.6 0.0 copy-done.1
  9.6 0.0 copy-done.2
  9.6 0.5 bitcast_add_fusion.src_ref
  10.1 27.9 %all-to-all-done = bf16[8,2,256,256]{3,2,1,0:T(8,128)(2,1)S(1)} async-done(((bf16[8,2,256,256]{3,2,1,0:T(8,128)(2,1)}), bf16[8,2,256,256]{3,2,1,0:T(8,128)(2,1)S(1)}, u32[]{:S(2)}, u32[]{:S(2)}) %all-to-all-start) | async-done | bytes 2097184 | tf_op jit(solution)/shard_map/all_to_all | solution.py:52
  38.1 0.0 copy-start
  38.1 1.3 %copy-done = bf16[8,2,256,256]{3,2,1,0:T(8,128)(2,1)} copy-done((bf16[8,2,256,256]{3,2,1,0:T(8,128)(2,1)}, bf16[8,2,256,256]{3,2,1,0:T(8,128)(2,1)S(1)}, u32[]{:S(2)}) %copy-start) | copy-done | bytes 2097176
  39.4 14.3 %shard_map.64 = f32[16,256,256]{2,1,0:T(8,128)} custom-call(s32[64]{0:T(128)} %bitcast_add_fusion.src_ref, s32[64]{0:T(128)} %tgt_ref.1, bf16[16,256,256]{2,1,0:T(8,128)(2,1)} %bitcast.9, bf16[64,256,256]{2,1,0:T(8,128)(2,1)} %left_ref.1, bf16[64,256,256]{2,1,0:T(8,128)(2,1)} %right_ref.1), custom_call_target="tpu_custom_call" | custom-call | tf_op jit(solution)/shard_map/pallas_call | solution.py:37
  53.7 2.5 %copy.10 = f32[64,2,32,256]{3,2,0,1:T(8,128)S(1)} copy(f32[64,2,32,256]{3,2,1,0:T(8,128)} %bitcast.8) | data formatting | bytes 8388608 | tf_op jit(solution)/shard_map/reshape;reshape | solution.py:58
  56.2 8.2 %all_to_all.15 = f32[2,64,32,256]{3,2,1,0:T(8,128)} all-to-all(f32[2,64,32,256]{3,2,1,0:T(8,128)S(1)} %bitcast.7), channel_id=1, replica_groups=mesh['y'=4,'xh'=2,'z'=4,'xl'=2,'c'=2] {'c'}, dimensions={0} | all-to-all | bytes 8388608 | tf_op jit(solution)/shard_map/all_to_all | solution.py:59
  64.4 2.8 %reduce_sum.18 = f32[64,32,256]{2,1,0:T(8,128)S(1)} reduce(f32[2,64,32,256]{3,2,1,0:T(8,128)} %all_to_all.15, f32[]{:T(128)} %constant.1.clone.1), dimensions={0}, to_apply=%region_0.0 | reduce | flops 524288 | bytes 6291460 | tf_op jit(solution)/shard_map/reduce_sum | solution.py:59
  67.2 37.1 %all_to_all.16 = f32[64,32,256]{2,1,0:T(8,128)} all-to-all(f32[64,32,256]{2,1,0:T(8,128)S(1)} %reduce_sum.18), channel_id=1, replica_groups=mesh['y'=4,'xh'=2,'z'=4,'xl'=2,'c'=2] {'y','xh','z','xl'}, dimensions={0} | all-to-all | bytes 4194304 | tf_op jit(solution)/shard_map/all_to_all | solution.py:60
  104.3 2.3 %reduce_sum.19 = f32[32,256]{1,0:T(8,128)} reduce(f32[64,32,256]{2,1,0:T(8,128)} %all_to_all.16, f32[]{:T(128)} %constant.1.clone.1), dimensions={0}, to_apply=%region_1.0 | reduce | flops 516096 | bytes 2129924 | tf_op jit(solution)/shard_map/reduce_sum | solution.py:61
Async XLA Ops:
  0.0 9.6 %copy-start.1 = (s32[64]{0:T(128)S(1)}, s32[64]{0:T(128)}, u32[]{:S(2)}) copy-start(s32[64]{0:T(128)} %param.10) | copy-start | bytes 772
  0.0 9.6 %copy-start.2 = (s32[64,1]{0,1:T(1,128)S(1)}, s32[64,1]{0,1:T(1,128)}, u32[]{:S(2)}) copy-start(s32[64,1]{0,1:T(1,128)} %param.9) | copy-start | bytes 772
  2.5 35.5 %all-to-all-start = ((bf16[8,2,256,256]{3,2,1,0:T(8,128)(2,1)}), bf16[8,2,256,256]{3,2,1,0:T(8,128)(2,1)S(1)}, u32[]{:S(2)}, u32[]{:S(2)}) async-start(bf16[8,2,256,256]{3,2,1,0:T(8,128)(2,1)} %broadcast_in_dim.2), calls=%async_computation | async-start | bytes 4194304 | tf_op jit(solution)/shard_map/all_to_all | solution.py:52
  38.1 1.3 %copy-start = (bf16[8,2,256,256]{3,2,1,0:T(8,128)(2,1)}, bf16[8,2,256,256]{3,2,1,0:T(8,128)(2,1)S(1)}, u32[]{:S(2)}) copy-start(bf16[8,2,256,256]{3,2,1,0:T(8,128)(2,1)S(1)} %all-to-all-done) | copy-start | bytes 6291460

commit v3 on v2

--- a/solution.py
+++ b/solution.py
@@ -48,17 +48,25 @@
 
 
 def gather_blocks(wavefunction, n_blk):
-    copies = jnp.broadcast_to(wavefunction[None], (n_blk,) + wavefunction.shape)
+    core = lax.axis_index("c")
+    mine = lax.dynamic_index_in_dim(wavefunction, core, 0, keepdims=False)
+    copies = jnp.broadcast_to(mine[None], (n_blk,) + mine.shape)
     got = lax.all_to_all(copies, ("y", "xh"), 0, 0, tiled=True)
-    return got.reshape((-1,) + wavefunction.shape[1:])
+    other = lax.ppermute(got, "c", [(0, 1), (1, 0)])
+    low = jnp.where(core == 0, got, other)
+    high = jnp.where(core == 0, other, got)
+    return jnp.stack([low, high], 1).reshape((-1,) + wavefunction.shape[1:])
 
 
 def reduce_rows(stacked, n_core, n_rest):
     rows = stacked.shape[0] // (n_core * n_rest)
-    y = stacked.reshape(n_rest, n_core, rows, stacked.shape[1]).transpose(1, 0, 2, 3)
-    y = lax.all_to_all(y, "c", 0, 0, tiled=True).reshape(n_core, n_rest, rows, -1).sum(0)
+    y = stacked.reshape(n_rest, n_core, rows, stacked.shape[1])
+    core = lax.axis_index("c")
+    mine = jnp.where(core == 0, y[:, 0], y[:, 1])
+    other = jnp.where(core == 0, y[:, 1], y[:, 0])
+    y = mine + lax.ppermute(other, "c", [(0, 1), (1, 0)])
     y = lax.all_to_all(y, ("y", "xh", "z", "xl"), 0, 0, tiled=True)
-    return y.reshape(n_rest, rows, -1).sum(0)
+    return y.sum(0)
 
 
 def on_device(wavefunction, left_terms, right_terms, term_slab, term_sector, term_target):

time: 107 us -> 89.9 us (0.84)
  waiting for transfers between devices: 27.9 us -> 6.16 us
  blocking collectives: 45.3 us -> 61.2 us
  starting transfers between devices: 7.04 us -> 0.22 us
  local copies, waits for them, and re-layouts: 6.37 us -> 1.04 us
    all_to_all x1 -> x0, waiting for transfers between devices: 27.9 us -> none  [gather_blocks(): got = lax.all_to_all(copies, ('y', 'xh'), 0, 0, tiled=True)]
    all_to_all x1, blocking collectives: 8.17 us -> 24 us  [gather_blocks(): got = lax.all_to_all(copies, ('y', 'xh'), 0, 0, tiled=True)]
    all_to_all x1 -> x0, starting transfers between devices: 7.04 us -> none  [gather_blocks(): got = lax.all_to_all(copies, ('y', 'xh'), 0, 0, tiled=True)]
    ppermute x0 -> x2, waiting for transfers between devices: none -> 6.16 us  [the longest x1 4.02 us: reduce_rows(): y = mine + lax.ppermute(other, 'c', [(0, 1), (1, 0)])]
    reduce_sum x2 -> x1, other arithmetic: 5.13 us -> 0.75 us  [reduce_rows(): return y.sum(0)]
    select_n x0 -> x1, other arithmetic: none -> 2.84 us  [reduce_rows(): other = jnp.where(core == 0, y[:, 1], y[:, 0])]
    another operation x1 -> x0, local copies, waits for them, and re-layouts: 2.5 us -> none  [reduce_rows(): stacked.reshape(n_rest, n_core, rows, stacked.shape[1])]
    broadcast_in_dim x1 -> x2, local copies, waits for them, and re-layouts: 2.53 us -> 0.08 us  [gather_blocks(): copies = jnp.broadcast_to(mine[None], (n_blk,) + mine.shape)]
  transfers between devices with their start and end apart: 1 -> 2, of which waited for: 1 -> 2; matrix products, arithmetic and copies ran while one was open for 0% -> 1% of each run, Pallas kernels for 0% -> 0%
where the time goes in v3:
time: 89.9 us; the launch traced here: 89.6 us
  blocking collectives  61.2 us (68%)
  Pallas kernels  14.3 us (16%)
  other arithmetic  6.62 us (7%)
  waiting for transfers between devices  6.16 us (7%)
  local copies, waits for them, and re-layouts  1.04 us (1%)
    all_to_all x1, blocking collectives, reduce_rows(): y = lax.all_to_all(y, ('y', 'xh', 'z', 'xl'), 0, 0, tiled=True)  37.1 us
    all_to_all x1, blocking collectives, gather_blocks(): got = lax.all_to_all(copies, ('y', 'xh'), 0, 0, tiled=True)  24 us
    pallas_call x1, Pallas kernels, add_terms(): pl.pallas_call(sigma_kernel, out_shape=jax.ShapeDtypeStruct((sectors, wid...  14.3 us
    ppermute x1, waiting for transfers between devices, reduce_rows(): y = mine + lax.ppermute(other, 'c', [(0, 1), (1, 0)])  4.02 us
    select_n x1, other arithmetic, reduce_rows(): other = jnp.where(core == 0, y[:, 1], y[:, 0])  2.84 us
    ppermute x1, waiting for transfers between devices, gather_blocks(): other = lax.ppermute(got, 'c', [(0, 1), (1, 0)])  2.13 us
  transfers between devices with their start and end apart: 2, of which 2 were waited for; matrix products, arithmetic and copies ran while one was open for 1% of the time, Pallas kernels for 0%

profile of v3, /device:TPU:0, one launch (start us, length us, event | category | flops | bytes accessed | tf_op | source)
XLA Modules:
  0.0 89.6 jit_solution(18152948673629348300)
XLA Ops:
  0.0 0.0 copy-start
  0.0 0.0 copy-start.2
  0.0 0.0 copy-start.3
  0.0 0.9 %copy-done = bf16[2,256,256]{2,1,0:T(8,128)(2,1)S(1)} copy-done((bf16[2,256,256]{2,1,0:T(8,128)(2,1)S(1)}, bf16[2,256,256]{2,1,0:T(8,128)(2,1)}, u32[]{:S(2)}) %copy-start) | copy-done | bytes 262168
  1.0 0.1 broadcast_in_dim.9
  1.0 24.0 %all_to_all.10 = bf16[8,256,256]{2,1,0:T(8,128)(2,1)S(1)} all-to-all(bf16[8,256,256]{2,1,0:T(8,128)(2,1)S(1)} %broadcast_in_dim.9), channel_id=1, replica_groups=mesh['y'=4,'xh'=2,'z'=4,'xl'=2,'c'=2] {'y','xh'}, dimensions={0} | all-to-all | bytes 2097152 | tf_op jit(solution)/shard_map/all_to_all | solution.py:54
  25.1 0.0 collective-permute-start
  25.1 0.0 copy-done.2
  25.1 0.0 copy-done.3
  25.1 0.5 bitcast_add_fusion.src_ref
  25.6 2.1 %collective-permute-done = bf16[8,256,256]{2,1,0:T(8,128)(2,1)S(1)} collective-permute-done((bf16[8,256,256]{2,1,0:T(8,128)(2,1)S(1)}, bf16[8,256,256]{2,1,0:T(8,128)(2,1)S(1)}, u32[]{:S(2)}, u32[]{:S(2)}) %collective-permute-start) | collective-permute-done | bytes 1048608 | tf_op jit(solution)/shard_map/ppermute | solution.py:55
  27.7 0.1 select_bitcast_fusion.2
  27.9 1.5 %pad_maximum_fusion = bf16[8,2,256,256]{3,2,1,0:T(8,128)(2,1)} fusion(bf16[8,1,256,256]{3,2,1,0:T(8,128)(2,1)S(1)} %get-tuple-element.6, bf16[8,1,256,256]{3,2,1,0:T(8,128)(2,1)S(1)} %get-tuple-element.5), kind=kLoop, calls=%fused_computation | loop fusion | flops 1048576 | bytes 4194304 | tf_op jit(solution)/shard_map/stack | solution.py:58
  29.4 14.3 %shard_map.64 = f32[16,256,256]{2,1,0:T(8,128)} custom-call(s32[64]{0:T(128)} %bitcast_add_fusion.src_ref, s32[64]{0:T(128)} %tgt_ref.1, bf16[16,256,256]{2,1,0:T(8,128)(2,1)} %bitcast.32, bf16[64,256,256]{2,1,0:T(8,128)(2,1)} %left_ref.1, bf16[64,256,256]{2,1,0:T(8,128)(2,1)} %right_ref.1), custom_call_target="tpu_custom_call" | custom-call | tf_op jit(solution)/shard_map/pallas_call | solution.py:37
  43.7 0.0 copy-start.1
  43.7 2.8 %select_bitcast_fusion = f32[64,32,256]{2,1,0:T(8,128)S(1)} fusion(f32[64,2,32,256]{3,2,1,0:T(8,128)} %bitcast.30, pred[]{:T(512)S(6)} %eq.2), kind=kLoop, calls=%fused_computation.4 | loop fusion | flops 524288 | bytes 6291457 | tf_op jit(solution)/shard_map/jit(_where)/select_n | solution.py:66
  46.6 0.2 collective-permute-start.1
  46.8 4.0 %collective-permute-done.1 = f32[64,32,256]{2,1,0:T(8,128)S(1)} collective-permute-done((f32[64,32,256]{2,1,0:T(8,128)S(1)}, f32[64,32,256]{2,1,0:T(8,128)S(1)}, u32[]{:S(2)}, u32[]{:S(2)}) %collective-permute-start.1) | collective-permute-done | bytes 2097184 | tf_op jit(solution)/shard_map/ppermute | solution.py:67
  50.8 0.0 copy-done.1
  50.8 0.9 fusion.1
  51.7 37.1 %all_to_all.11 = f32[64,32,256]{2,1,0:T(8,128)S(1)} all-to-all(f32[64,32,256]{2,1,0:T(8,128)S(1)} %fusion.1), channel_id=1, replica_groups=mesh['y'=4,'xh'=2,'z'=4,'xl'=2,'c'=2] {'y','xh','z','xl'}, dimensions={0} | all-to-all | bytes 4194304 | tf_op jit(solution)/shard_map/all_to_all | solution.py:68
  88.8 0.8 reduce_sum.9
  (1 shorter events, 0.0 us)
Async XLA Ops:
  0.0 1.0 %copy-start = (bf16[2,256,256]{2,1,0:T(8,128)(2,1)S(1)}, bf16[2,256,256]{2,1,0:T(8,128)(2,1)}, u32[]{:S(2)}) copy-start(bf16[2,256,256]{2,1,0:T(8,128)(2,1)} %param.6) | copy-start | bytes 786436
  0.0 25.1 %copy-start.2 = (s32[64]{0:T(128)S(1)}, s32[64]{0:T(128)}, u32[]{:S(2)}) copy-start(s32[64]{0:T(128)} %param.10) | copy-start | bytes 772
  0.0 25.1 %copy-start.3 = (s32[64,1]{0,1:T(1,128)S(1)}, s32[64,1]{0,1:T(1,128)}, u32[]{:S(2)}) copy-start(s32[64,1]{0,1:T(1,128)} %param.9) | copy-start | bytes 772
  25.1 2.7 %collective-permute-start = (bf16[8,256,256]{2,1,0:T(8,128)(2,1)S(1)}, bf16[8,256,256]{2,1,0:T(8,128)(2,1)S(1)}, u32[]{:S(2)}, u32[]{:S(2)}) collective-permute-start(bf16[8,256,256]{2,1,0:T(8,128)(2,1)S(1)} %all_to_all.10), channel_id=1, source_target_pairs={{0,1},{1,0},{2,3},{3,2},{4,5},{5,4},{6,7},{7,6},{8,9},{9,8},{10,11... | collective-permute-start | bytes 3145736 | tf_op jit(solution)/shard_map/ppermute | solution.py:55
  43.7 7.1 %copy-start.1 = (f32[16,256,256]{2,1,0:T(8,128)S(1)}, f32[16,256,256]{2,1,0:T(8,128)}, u32[]{:S(2)}) copy-start(f32[16,256,256]{2,1,0:T(8,128)} %shard_map.64) | copy-start | bytes 12582916
  46.6 4.2 %collective-permute-start.1 = (f32[64,32,256]{2,1,0:T(8,128)S(1)}, f32[64,32,256]{2,1,0:T(8,128)S(1)}, u32[]{:S(2)}, u32[]{:S(2)}) collective-permute-start(f32[64,32,256]{2,1,0:T(8,128)S(1)} %select_bitcast_fusion), channel_id=1, source_target_pairs={{0,1},{1,0},{2,3},{3,2},{4,5},{5,4},{6,7},{7,6},{8,9},{9,8},{10,11... | collective-permute-start | bytes 6291464 | tf_op jit(solution)/shard_map/ppermute | solution.py:67

commit v4 on v2

v4 whole, which is shorter than its diff:
```python
import jax
import jax.numpy as jnp
from jax import lax
from jax.experimental import pallas as pl
from jax.experimental.pallas import tpu as pltpu
from jax.sharding import Mesh
from jax.sharding import PartitionSpec as P

PHYS = ("y", "xh", "z", "xl", "c")
TERM_BLOCK = 8


def sigma_kernel(core_ref, slab_ref, sector_ref, tgt_ref, own_ref, swapped_ref,
                 left_ref, right_ref, out_ref):
    step = pl.program_id(0)
    core = core_ref[0]
    n_core = out_ref.shape[0]
    bands = out_ref.shape[2]
    band = out_ref.shape[3]

    @pl.when(step == 0)
    def _():
        out_ref[...] = jnp.zeros_like(out_ref)

    for j in range(TERM_BLOCK):
        t = step * TERM_BLOCK + j
        slab = slab_ref[t]
        target = tgt_ref[t]

        def accumulate(psi_ref, j=j, slab=slab, target=target):
            left_part = jnp.dot(
                left_ref[j], psi_ref[slab], preferred_element_type=jnp.float32
            ).astype(jnp.bfloat16)
            term_image = lax.dot_general(
                left_part, right_ref[j], (((1,), (1,)), ((), ())),
                preferred_element_type=jnp.float32,
            )
            for q in range(bands):
                for cc in range(n_core):
                    row = (q * n_core + cc) * band
                    slot = jnp.where(cc == core, 0, 1)
                    out_ref[slot, target, q] += term_image[row:row + band]

        own = sector_ref[t] == core

        @pl.when(own)
        def _():
            accumulate(own_ref)

        @pl.when(jnp.logical_not(own))
        def _():
            accumulate(swapped_ref)


def add_terms(own, swapped, left_terms, right_terms, slab, sector, targets, core, n_core, band):
    n_slab, width, _ = own.shape
    sectors = n_slab * n_core
    bands = width // (band * n_core)
    n_terms = left_terms.shape[0]
    whole = pl.BlockSpec((n_slab, width, width), lambda i, *_: (0, 0, 0))
    per_step = pl.BlockSpec((TERM_BLOCK, width, width), lambda i, *_: (i, 0, 0))
    out_shape = (n_core, sectors, bands, band, width)
    return pl.pallas_call(
        sigma_kernel,
        out_shape=jax.ShapeDtypeStruct(out_shape, jnp.float32),
        grid_spec=pltpu.PrefetchScalarGridSpec(
            num_scalar_prefetch=4,
            grid=(n_terms // TERM_BLOCK,),
            in_specs=[whole, whole, per_step, per_step],
            out_specs=pl.BlockSpec(out_shape, lambda i, *_: (0,) * len(out_shape)),
        ),
        compiler_params=pltpu.CompilerParams(dimension_semantics=("arbitrary",)),
    )(core, slab, sector, targets, own, swapped, left_terms, right_terms)


def gather_blocks(wavefunction, n_blk):
    core = lax.axis_index("c")
    mine = lax.dynamic_index_in_dim(wavefunction, core, 0, keepdims=False)
    copies = jnp.broadcast_to(mine[None], (n_blk,) + mine.shape)
    own = lax.all_to_all(copies, ("y", "xh"), 0, 0, tiled=True)
    swapped = lax.ppermute(own, "c", [(0, 1), (1, 0)])
    return own, swapped


def on_device(wavefunction, left_terms, right_terms, term_slab, term_sector, term_target):
    n_blk = lax.axis_size(("y", "xh"))
    n_core = lax.axis_size("c")
    n_rest = lax.axis_size(("y", "xh", "z", "xl"))
    width = wavefunction.shape[1]
    band = wavefunction.shape[0] * n_blk * width // (n_core * n_rest)
    core = lax.axis_index("c").astype(jnp.int32).reshape(1)
    own, swapped = gather_blocks(wavefunction, n_blk)
    parts = add_terms(
        own, swapped, left_terms, right_terms, term_slab[:, 0], term_sector, term_target,
        core, n_core, band,
    )
    mine = parts[0].reshape(n_rest, band, width)
    other = parts[1].reshape(n_rest, band, width)
    summed = mine + lax.ppermute(other, "c", [(0, 1), (1, 0)])
    got = lax.all_to_all(summed, ("y", "xh", "z", "xl"), 0, 0, tiled=True)
    return got.sum(0)


def solution(mesh):
    blk, terms = mesh.axis_names
    n_blk, n_terms = mesh.shape[blk], mesh.shape[terms]
    n_core = 2
    phys = Mesh(
        mesh.devices.reshape(n_blk // 2, 2, n_terms // (2 * n_core), 2, n_core), PHYS
    )
    wave = ("y", "xh")
    spread = PHYS
    placed = (
        P(wave, None, None),
        P(spread, None, None),
        P(spread, None, None),
        P(spread, None),
        P(spread),
        P(spread),
    )
    return jax.shard_map(
        on_device, mesh=phys, in_specs=placed, out_specs=P(spread, None), check_vma=False
    )
```

time: 107 us -> 101 us (0.944)
  waiting for transfers between devices: 27.9 us -> 6.69 us
  blocking collectives: 45.3 us -> 61.2 us
  Pallas kernels: 14.3 us -> 27.2 us
  starting transfers between devices: 7.04 us -> 0.21 us
  other arithmetic: 5.65 us -> 1.24 us
  local copies, waits for them, and re-layouts: 6.37 us -> 4.56 us
    all_to_all x1 -> x0, waiting for transfers between devices: 27.9 us -> none  [gather_blocks(): got = lax.all_to_all(copies, ('y', 'xh'), 0, 0, tiled=True)]
    all_to_all x2, blocking collectives: 45.3 us -> 61.2 us  [the longest x1 37.1 us: on_device(): got = lax.all_to_all(summed, ('y', 'xh', 'z', 'xl'), 0, 0, tiled=True)]
    pallas_call x1, Pallas kernels: 14.3 us -> 27.2 us  [add_terms(): pl.pallas_call(sigma_kernel, out_shape=jax.ShapeDtypeStruct(out_shape, jn...]
    all_to_all x1 -> x0, starting transfers between devices: 7.04 us -> none  [gather_blocks(): got = lax.all_to_all(copies, ('y', 'xh'), 0, 0, tiled=True)]
    ppermute x0 -> x2, waiting for transfers between devices: none -> 6.69 us  [the longest x1 4.03 us: on_device(): summed = mine + lax.ppermute(other, 'c', [(0, 1), (1, 0)])]
    reduce_sum x2 -> x1, other arithmetic: 5.13 us -> 0.75 us  [on_device(): return got.sum(0)]
    slice x0 -> x1, local copies, waits for them, and re-layouts: none -> 2.54 us  [on_device(): mine = parts[0].reshape(n_rest, band, width)]
    another operation x1 -> x0, local copies, waits for them, and re-layouts: 2.5 us -> none  [reduce_rows(): stacked.reshape(n_rest, n_core, rows, stacked.shape[1])]
  transfers between devices with their start and end apart: 1 -> 2, of which waited for: 1 -> 2; matrix products, arithmetic and copies ran while one was open for 0% -> 0% of each run, Pallas kernels for 0% -> 0%
where the time goes in v4:
time: 101 us
  blocking collectives  61.2 us (61%)
  Pallas kernels  27.2 us (27%)
  waiting for transfers between devices  6.69 us (7%)
  local copies, waits for them, and re-layouts  4.56 us (5%)
  other arithmetic  1.24 us (1%)
    all_to_all x1, blocking collectives, on_device(): got = lax.all_to_all(summed, ('y', 'xh', 'z', 'xl'), 0, 0, tiled=True)  37.1 us
    pallas_call x1, Pallas kernels, add_terms(): pl.pallas_call(sigma_kernel, out_shape=jax.ShapeDtypeStruct(out_shape, jn...  27.2 us
    all_to_all x1, blocking collectives, gather_blocks(): own = lax.all_to_all(copies, ('y', 'xh'), 0, 0, tiled=True)  24 us
    ppermute x1, waiting for transfers between devices, on_device(): summed = mine + lax.ppermute(other, 'c', [(0, 1), (1, 0)])  4.03 us
    ppermute x1, waiting for transfers between devices, gather_blocks(): swapped = lax.ppermute(own, 'c', [(0, 1), (1, 0)])  2.66 us
    slice x1, local copies, waits for them, and re-layouts, on_device(): mine = parts[0].reshape(n_rest, band, width)  2.54 us
  transfers between devices with their start and end apart: 2, of which 2 were waited for; matrix products, arithmetic and copies ran while one was open for 0% of the time, Pallas kernels for 0%

profile of v4, /device:TPU:0, one launch (start us, length us, event | category | flops | bytes accessed | tf_op | source)
XLA Modules:
  0.0 101.1 jit_solution(1901994680579325280)
XLA Ops:
  0.0 0.0 copy-start
  0.0 0.9 copy-done
  1.0 0.1 broadcast_in_dim.9
  1.0 24.0 %all_to_all.10.own_ref = bf16[8,256,256]{2,1,0:T(8,128)(2,1)S(1)} all-to-all(bf16[8,256,256]{2,1,0:T(8,128)(2,1)S(1)} %broadcast_in_dim.9), channel_id=1, replica_groups=mesh['y'=4,'xh'=2,'z'=4,'xl'=2,'c'=2] {'y','xh'}, dimensions={0} | all-to-all | bytes 2097152 | tf_op jit(solution)/shard_map/all_to_all | solution.py:80
  25.1 0.0 copy-start.1
  25.1 0.0 collective-permute-start
  25.1 2.7 %collective-permute-done.swapped_ref = bf16[8,256,256]{2,1,0:T(8,128)(2,1)S(1)} collective-permute-done((bf16[8,256,256]{2,1,0:T(8,128)(2,1)S(1)}, bf16[8,256,256]{2,1,0:T(8,128)(2,1)S(1)}, u32[]{:S(2)}, u32[]{:S(2)}) %collective-permute-start) | collective-permute-done | bytes 1048608 | tf_op jit(solution)/shard_map/ppermute | solution.py:81
  27.7 0.0 copy-start.2
  27.7 0.0 copy-done.1
  27.8 1.0 copy-done.2
  28.7 27.2 %shard_map.64 = f32[2,16,4,32,256]{4,3,2,1,0:T(8,128)} custom-call(s32[1]{0:T(128)} %bitcast.core_ref, s32[64]{0:T(128)} %bitcast.8, s32[64]{0:T(128)} %sector_ref.1, s32[64]{0:T(128)} %tgt_ref.1, bf16[8,256,256]{2,1,0:T(8,128)(2,1)} %copy-done.1, bf16[8,256,256]{2,1,0:T(8,128)(2,1)} %copy-done.2, bf16[64,256,256]{2,1,0:T(8,128)(2,1)} %left_ref.1, ...), custom_call_target="tpu_custom_call" | custom-call | tf_op jit(solution)/shard_map/pallas_call | solution.py:63
  56.0 2.5 %fusion = (f32[1,16,4,32,256]{4,3,2,1,0:T(8,128)S(1)}, f32[1,16,4,32,256]{4,3,2,1,0:T(8,128)S(1)}) fusion(f32[2,16,4,32,256]{4,3,2,1,0:T(8,128)} %shard_map.64), kind=kLoop, calls=%fused_computation.2 | loop fusion | bytes 8388608 | tf_op jit(solution)/shard_map/slice | solution.py:97
  58.5 0.2 collective-permute-start.1
  58.7 4.0 %collective-permute-done.1 = f32[64,32,256]{2,1,0:T(8,128)S(1)} collective-permute-done((f32[64,32,256]{2,1,0:T(8,128)S(1)}, f32[64,32,256]{2,1,0:T(8,128)S(1)}, u32[]{:S(2)}, u32[]{:S(2)}) %collective-permute-start.1) | collective-permute-done | bytes 2097184 | tf_op jit(solution)/shard_map/ppermute | solution.py:99
  62.7 0.5 bitcast_add_fusion
  63.2 37.1 %all_to_all.11 = f32[64,32,256]{2,1,0:T(8,128)S(1)} all-to-all(f32[64,32,256]{2,1,0:T(8,128)S(1)} %bitcast_add_fusion), channel_id=1, replica_groups=mesh['y'=4,'xh'=2,'z'=4,'xl'=2,'c'=2] {'y','xh','z','xl'}, dimensions={0} | all-to-all | bytes 4194304 | tf_op jit(solution)/shard_map/all_to_all | solution.py:100
  100.3 0.8 reduce_sum.9
  (1 shorter events, 0.0 us)
Async XLA Ops:
  0.0 1.0 copy-start
  25.1 2.7 %copy-start.1 = (bf16[8,256,256]{2,1,0:T(8,128)(2,1)}, bf16[8,256,256]{2,1,0:T(8,128)(2,1)S(1)}, u32[]{:S(2)}) copy-start(bf16[8,256,256]{2,1,0:T(8,128)(2,1)S(1)} %all_to_all.10.own_ref) | copy-start | bytes 3145732
  25.1 2.7 %collective-permute-start = (bf16[8,256,256]{2,1,0:T(8,128)(2,1)S(1)}, bf16[8,256,256]{2,1,0:T(8,128)(2,1)S(1)}, u32[]{:S(2)}, u32[]{:S(2)}) collective-permute-start(bf16[8,256,256]{2,1,0:T(8,128)(2,1)S(1)} %all_to_all.10.own_ref), channel_id=1, source_target_pairs={{0,1},{1,0},{2,3},{3,2},{4,5},{5,4},{6,7},{7,6},{8,9},{9,8},{10,11... | collective-permute-start | bytes 3145736 | tf_op jit(solution)/shard_map/ppermute | solution.py:81
  27.7 1.0 copy-start.2
  58.5 4.2 %collective-permute-start.1 = (f32[64,32,256]{2,1,0:T(8,128)S(1)}, f32[64,32,256]{2,1,0:T(8,128)S(1)}, u32[]{:S(2)}, u32[]{:S(2)}) collective-permute-start(f32[64,32,256]{2,1,0:T(8,128)S(1)} %bitcast.7), channel_id=1, source_target_pairs={{0,1},{1,0},{2,3},{3,2},{4,5},{5,4},{6,7},{7,6},{8,9},{9,8},{10,11... | collective-permute-start | bytes 6291464 | tf_op jit(solution)/shard_map/ppermute | solution.py:99

commit v5 on v3

--- a/solution.py
+++ b/solution.py
@@ -7,7 +7,7 @@
 from jax.sharding import PartitionSpec as P
 
 PHYS = ("y", "xh", "z", "xl", "c")
-TERM_BLOCK = 8
+TERM_BLOCK = 32
 
 
 def sigma_kernel(src_ref, tgt_ref, psi_ref, left_ref, right_ref, out_ref):

time: 89.9 us -> 87.3 us (0.971)
  Pallas kernels: 14.3 us -> 11.9 us
    pallas_call x1, Pallas kernels: 14.3 us -> 11.9 us  [add_terms(): pl.pallas_call(sigma_kernel, out_shape=jax.ShapeDtypeStruct((sectors, wid...]
where the time goes in v5:
time: 87.3 us; the launch traced here: 87.1 us
  blocking collectives  61.2 us (70%)
  Pallas kernels  11.9 us (14%)
  other arithmetic  6.62 us (8%)
  waiting for transfers between devices  6.16 us (7%)
  local copies, waits for them, and re-layouts  1.04 us (1%)
    all_to_all x1, blocking collectives, reduce_rows(): y = lax.all_to_all(y, ('y', 'xh', 'z', 'xl'), 0, 0, tiled=True)  37.1 us
    all_to_all x1, blocking collectives, gather_blocks(): got = lax.all_to_all(copies, ('y', 'xh'), 0, 0, tiled=True)  24 us
    pallas_call x1, Pallas kernels, add_terms(): pl.pallas_call(sigma_kernel, out_shape=jax.ShapeDtypeStruct((sectors, wid...  11.9 us
    ppermute x1, waiting for transfers between devices, reduce_rows(): y = mine + lax.ppermute(other, 'c', [(0, 1), (1, 0)])  4.02 us
    select_n x1, other arithmetic, reduce_rows(): other = jnp.where(core == 0, y[:, 1], y[:, 0])  2.84 us
    ppermute x1, waiting for transfers between devices, gather_blocks(): other = lax.ppermute(got, 'c', [(0, 1), (1, 0)])  2.13 us
  transfers between devices with their start and end apart: 2, of which 2 were waited for; matrix products, arithmetic and copies ran while one was open for 1% of the time, Pallas kernels for 0%

profile of v5, /device:TPU:0, one launch (start us, length us, event | category | flops | bytes accessed | tf_op | source)
XLA Modules:
  0.0 87.1 jit_solution(3066902996538340958)
XLA Ops:
  0.0 0.0 copy-start
  0.0 0.0 copy-start.2
  0.0 0.0 copy-start.3
  0.0 0.9 %copy-done = bf16[2,256,256]{2,1,0:T(8,128)(2,1)S(1)} copy-done((bf16[2,256,256]{2,1,0:T(8,128)(2,1)S(1)}, bf16[2,256,256]{2,1,0:T(8,128)(2,1)}, u32[]{:S(2)}) %copy-start) | copy-done | bytes 262168
  1.0 0.1 broadcast_in_dim.9
  1.0 24.0 %all_to_all.10 = bf16[8,256,256]{2,1,0:T(8,128)(2,1)S(1)} all-to-all(bf16[8,256,256]{2,1,0:T(8,128)(2,1)S(1)} %broadcast_in_dim.9), channel_id=1, replica_groups=mesh['y'=4,'xh'=2,'z'=4,'xl'=2,'c'=2] {'y','xh'}, dimensions={0} | all-to-all | bytes 2097152 | tf_op jit(solution)/shard_map/all_to_all | solution.py:54
  25.1 0.0 collective-permute-start
  25.1 0.0 copy-done.2
  25.1 0.0 copy-done.3
  25.1 0.5 bitcast_add_fusion.src_ref
  25.6 2.1 %collective-permute-done = bf16[8,256,256]{2,1,0:T(8,128)(2,1)S(1)} collective-permute-done((bf16[8,256,256]{2,1,0:T(8,128)(2,1)S(1)}, bf16[8,256,256]{2,1,0:T(8,128)(2,1)S(1)}, u32[]{:S(2)}, u32[]{:S(2)}) %collective-permute-start) | collective-permute-done | bytes 1048608 | tf_op jit(solution)/shard_map/ppermute | solution.py:55
  27.7 0.1 select_bitcast_fusion.2
  27.9 1.5 %pad_maximum_fusion = bf16[8,2,256,256]{3,2,1,0:T(8,128)(2,1)} fusion(bf16[8,1,256,256]{3,2,1,0:T(8,128)(2,1)S(1)} %get-tuple-element.6, bf16[8,1,256,256]{3,2,1,0:T(8,128)(2,1)S(1)} %get-tuple-element.5), kind=kLoop, calls=%fused_computation | loop fusion | flops 1048576 | bytes 4194304 | tf_op jit(solution)/shard_map/stack | solution.py:58
  29.4 11.9 %shard_map.64 = f32[16,256,256]{2,1,0:T(8,128)} custom-call(s32[64]{0:T(128)} %bitcast_add_fusion.src_ref, s32[64]{0:T(128)} %tgt_ref.1, bf16[16,256,256]{2,1,0:T(8,128)(2,1)} %bitcast.32, bf16[64,256,256]{2,1,0:T(8,128)(2,1)} %left_ref.1, bf16[64,256,256]{2,1,0:T(8,128)(2,1)} %right_ref.1), custom_call_target="tpu_custom_call" | custom-call | tf_op jit(solution)/shard_map/pallas_call | solution.py:37
  41.3 0.0 copy-start.1
  41.3 2.8 %select_bitcast_fusion = f32[64,32,256]{2,1,0:T(8,128)S(1)} fusion(f32[64,2,32,256]{3,2,1,0:T(8,128)} %bitcast.30, pred[]{:T(512)S(6)} %eq.2), kind=kLoop, calls=%fused_computation.4 | loop fusion | flops 524288 | bytes 6291457 | tf_op jit(solution)/shard_map/jit(_where)/select_n | solution.py:66
  44.1 0.2 collective-permute-start.1
  44.4 4.0 %collective-permute-done.1 = f32[64,32,256]{2,1,0:T(8,128)S(1)} collective-permute-done((f32[64,32,256]{2,1,0:T(8,128)S(1)}, f32[64,32,256]{2,1,0:T(8,128)S(1)}, u32[]{:S(2)}, u32[]{:S(2)}) %collective-permute-start.1) | collective-permute-done | bytes 2097184 | tf_op jit(solution)/shard_map/ppermute | solution.py:67
  48.4 0.0 copy-done.1
  48.4 0.9 fusion.1
  49.3 37.1 %all_to_all.11 = f32[64,32,256]{2,1,0:T(8,128)S(1)} all-to-all(f32[64,32,256]{2,1,0:T(8,128)S(1)} %fusion.1), channel_id=1, replica_groups=mesh['y'=4,'xh'=2,'z'=4,'xl'=2,'c'=2] {'y','xh','z','xl'}, dimensions={0} | all-to-all | bytes 4194304 | tf_op jit(solution)/shard_map/all_to_all | solution.py:68
  86.4 0.8 reduce_sum.9
  (1 shorter events, 0.0 us)
Async XLA Ops:
  0.0 1.0 %copy-start = (bf16[2,256,256]{2,1,0:T(8,128)(2,1)S(1)}, bf16[2,256,256]{2,1,0:T(8,128)(2,1)}, u32[]{:S(2)}) copy-start(bf16[2,256,256]{2,1,0:T(8,128)(2,1)} %param.6) | copy-start | bytes 786436
  0.0 25.1 %copy-start.2 = (s32[64]{0:T(128)S(1)}, s32[64]{0:T(128)}, u32[]{:S(2)}) copy-start(s32[64]{0:T(128)} %param.10) | copy-start | bytes 772
  0.0 25.1 %copy-start.3 = (s32[64,1]{0,1:T(1,128)S(1)}, s32[64,1]{0,1:T(1,128)}, u32[]{:S(2)}) copy-start(s32[64,1]{0,1:T(1,128)} %param.9) | copy-start | bytes 772
  25.1 2.7 %collective-permute-start = (bf16[8,256,256]{2,1,0:T(8,128)(2,1)S(1)}, bf16[8,256,256]{2,1,0:T(8,128)(2,1)S(1)}, u32[]{:S(2)}, u32[]{:S(2)}) collective-permute-start(bf16[8,256,256]{2,1,0:T(8,128)(2,1)S(1)} %all_to_all.10), channel_id=1, source_target_pairs={{0,1},{1,0},{2,3},{3,2},{4,5},{5,4},{6,7},{7,6},{8,9},{9,8},{10,11... | collective-permute-start | bytes 3145736 | tf_op jit(solution)/shard_map/ppermute | solution.py:55
  41.3 7.1 %copy-start.1 = (f32[16,256,256]{2,1,0:T(8,128)S(1)}, f32[16,256,256]{2,1,0:T(8,128)}, u32[]{:S(2)}) copy-start(f32[16,256,256]{2,1,0:T(8,128)} %shard_map.64) | copy-start | bytes 12582916
  44.1 4.2 %collective-permute-start.1 = (f32[64,32,256]{2,1,0:T(8,128)S(1)}, f32[64,32,256]{2,1,0:T(8,128)S(1)}, u32[]{:S(2)}, u32[]{:S(2)}) collective-permute-start(f32[64,32,256]{2,1,0:T(8,128)S(1)} %select_bitcast_fusion), channel_id=1, source_target_pairs={{0,1},{1,0},{2,3},{3,2},{4,5},{5,4},{6,7},{7,6},{8,9},{9,8},{10,11... | collective-permute-start | bytes 6291464 | tf_op jit(solution)/shard_map/ppermute | solution.py:67

commit v6 on v5

v6 whole, which is shorter than its diff:
```python
import jax
import jax.numpy as jnp
from jax import lax
from jax.experimental import pallas as pl
from jax.experimental.pallas import tpu as pltpu
from jax.sharding import Mesh
from jax.sharding import PartitionSpec as P

PHYS = ("y", "xh", "z", "xl", "c")
TERM_BLOCK = 32


def sigma_kernel(core_ref, src_ref, tgt_ref, psi_ref, left_ref, right_ref, out_ref):
    step = pl.program_id(0)
    rows = out_ref.shape[1]

    @pl.when(step == 0)
    def _():
        out_ref[...] = jnp.zeros_like(out_ref)

    for j in range(TERM_BLOCK):
        t = step * TERM_BLOCK + j
        left_rows = left_ref[j].reshape(rows, left_ref.shape[-1])
        left_part = jnp.dot(
            left_rows, psi_ref[src_ref[t]], preferred_element_type=jnp.float32
        ).astype(jnp.bfloat16)
        term_image = lax.dot_general(
            left_part, right_ref[j], (((1,), (1,)), ((), ())),
            preferred_element_type=jnp.float32,
        )
        out_ref[tgt_ref[t]] += term_image


def add_terms(wave_blocks, left_bands, right_terms, sources, targets, core, other):
    sectors, width, _ = wave_blocks.shape
    n_terms, bands, n_core, band, _ = left_bands.shape
    rows = bands * band

    def pick(c):
        return (c + 1) % n_core if other else c

    whole = pl.BlockSpec((sectors, width, width), lambda i, *_: (0, 0, 0))
    per_step = pl.BlockSpec((TERM_BLOCK, width, width), lambda i, *_: (i, 0, 0))
    left_step = pl.BlockSpec(
        (TERM_BLOCK, bands, None, band, width), lambda i, c, *_: (i, 0, pick(c[0]), 0, 0)
    )
    out_spec = pl.BlockSpec((sectors, rows, width), lambda i, *_: (0, 0, 0))
    return pl.pallas_call(
        sigma_kernel,
        out_shape=jax.ShapeDtypeStruct((sectors, rows, width), jnp.float32),
        grid_spec=pltpu.PrefetchScalarGridSpec(
            num_scalar_prefetch=3,
            grid=(n_terms // TERM_BLOCK,),
            in_specs=[whole, left_step, per_step],
            out_specs=out_spec,
        ),
        compiler_params=pltpu.CompilerParams(dimension_semantics=("arbitrary",)),
    )(core, sources, targets, wave_blocks, left_bands, right_terms)


def gather_blocks(wavefunction, n_blk):
    core = lax.axis_index("c")
    mine = lax.dynamic_index_in_dim(wavefunction, core, 0, keepdims=False)
    copies = jnp.broadcast_to(mine[None], (n_blk,) + mine.shape)
    got = lax.all_to_all(copies, ("y", "xh"), 0, 0, tiled=True)
    other = lax.ppermute(got, "c", [(0, 1), (1, 0)])
    low = jnp.where(core == 0, got, other)
    high = jnp.where(core == 0, other, got)
    return jnp.stack([low, high], 1).reshape((-1,) + wavefunction.shape[1:])


def on_device(wavefunction, left_terms, right_terms, term_slab, term_sector, term_target):
    per_slab = wavefunction.shape[0]
    n_blk = lax.axis_size(("y", "xh"))
    n_core = lax.axis_size("c")
    n_rest = lax.axis_size(("y", "xh", "z", "xl"))
    width = wavefunction.shape[1]
    band = per_slab * n_blk * width // (n_core * n_rest)
    bands = width // (band * n_core)
    sources = term_slab[:, 0] * per_slab + term_sector
    core = lax.axis_index("c").astype(jnp.int32).reshape(1)
    gathered = gather_blocks(wavefunction, n_blk)
    left_bands = left_terms.reshape(left_terms.shape[0], bands, n_core, band, width)
    other = add_terms(gathered, left_bands, right_terms, sources, term_target, core, True)
    sent = lax.ppermute(other.reshape(n_rest, band, width), "c", [(0, 1), (1, 0)])
    mine = add_terms(gathered, left_bands, right_terms, sources, term_target, core, False)
    summed = mine.reshape(n_rest, band, width) + sent
    got = lax.all_to_all(summed, ("y", "xh", "z", "xl"), 0, 0, tiled=True)
    return got.sum(0)


def solution(mesh):
    blk, terms = mesh.axis_names
    n_blk, n_terms = mesh.shape[blk], mesh.shape[terms]
    n_core = 2
    phys = Mesh(
        mesh.devices.reshape(n_blk // 2, 2, n_terms // (2 * n_core), 2, n_core), PHYS
    )
    wave = ("y", "xh")
    spread = PHYS
    placed = (
        P(wave, None, None),
        P(spread, None, None),
        P(spread, None, None),
        P(spread, None),
        P(spread),
        P(spread),
    )
    return jax.shard_map(
        on_device, mesh=phys, in_specs=placed, out_specs=P(spread, None), check_vma=False
    )
```

time: 87.3 us -> 92.5 us (1.060)
  Pallas kernels: 11.9 us -> 22.7 us
  waiting for transfers between devices: 6.16 us -> 2.15 us
  other arithmetic: 6.62 us -> 4.9 us
    pallas_call x1 -> x2, Pallas kernels: 11.9 us -> 22.7 us  [add_terms(): pl.pallas_call(sigma_kernel, out_shape=jax.ShapeDtypeStruct((sectors, row...]
    ppermute x1, waiting for transfers between devices: 4.02 us -> 0.01 us  [on_device(): lax.ppermute(other.reshape(n_rest, band, width), 'c', [(0, 1), (1, 0)])]
    select_n x1 -> x0, other arithmetic: 2.84 us -> none  [reduce_rows(): other = jnp.where(core == 0, y[:, 1], y[:, 0])]
    add x1, other arithmetic: 0.87 us -> 1.98 us  [on_device(): summed = mine.reshape(n_rest, band, width) + sent]
  transfers between devices with their start and end apart: 2 -> 2, of which waited for: 2 -> 1; matrix products, arithmetic and copies ran while one was open for 1% -> 1% of each run, Pallas kernels for 0% -> 12%
where the time goes in v6:
time: 92.5 us; the launch traced here: 92.2 us
  blocking collectives  61.3 us (66%)
  Pallas kernels  22.7 us (25%)
  other arithmetic  4.9 us (5%)
  waiting for transfers between devices  2.15 us (2%)
  local copies, waits for them, and re-layouts  1.03 us (1%)
    all_to_all x1, blocking collectives, on_device(): got = lax.all_to_all(summed, ('y', 'xh', 'z', 'xl'), 0, 0, tiled=True)  37.2 us
    all_to_all x1, blocking collectives, gather_blocks(): got = lax.all_to_all(copies, ('y', 'xh'), 0, 0, tiled=True)  24 us
    pallas_call x2, Pallas kernels, add_terms(): pl.pallas_call(sigma_kernel, out_shape=jax.ShapeDtypeStruct((sectors, row...  22.7 us
    ppermute x1, waiting for transfers between devices, gather_blocks(): other = lax.ppermute(got, 'c', [(0, 1), (1, 0)])  2.14 us
    add x1, other arithmetic, on_device(): summed = mine.reshape(n_rest, band, width) + sent  1.98 us
  transfers between devices with their start and end apart: 2, of which 1 were waited for; matrix products, arithmetic and copies ran while one was open for 1% of the time, Pallas kernels for 12%

profile of v6, /device:TPU:0, one launch (start us, length us, event | category | flops | bytes accessed | tf_op | source)
XLA Modules:
  0.0 92.2 jit_solution(17359824319603988507)
XLA Ops:
  0.0 0.0 copy-start
  0.0 0.0 copy-start.1
  0.0 0.0 copy-start.2
  0.0 0.9 %copy-done = bf16[2,256,256]{2,1,0:T(8,128)(2,1)S(1)} copy-done((bf16[2,256,256]{2,1,0:T(8,128)(2,1)S(1)}, bf16[2,256,256]{2,1,0:T(8,128)(2,1)}, u32[]{:S(2)}) %copy-start) | copy-done | bytes 262168
  1.0 0.1 broadcast_in_dim.9
  1.0 24.0 %all_to_all.10 = bf16[8,256,256]{2,1,0:T(8,128)(2,1)S(1)} all-to-all(bf16[8,256,256]{2,1,0:T(8,128)(2,1)S(1)} %broadcast_in_dim.9), channel_id=1, replica_groups=mesh['y'=4,'xh'=2,'z'=4,'xl'=2,'c'=2] {'y','xh'}, dimensions={0} | all-to-all | bytes 2097152 | tf_op jit(solution)/shard_map/all_to_all | solution.py:65
  25.1 0.0 collective-permute-start
  25.1 0.0 copy-done.1
  25.1 0.0 copy-done.2
  25.1 0.5 bitcast_add_fusion.src_ref
  25.6 2.1 %collective-permute-done = bf16[8,256,256]{2,1,0:T(8,128)(2,1)S(1)} collective-permute-done((bf16[8,256,256]{2,1,0:T(8,128)(2,1)S(1)}, bf16[8,256,256]{2,1,0:T(8,128)(2,1)S(1)}, u32[]{:S(2)}, u32[]{:S(2)}) %collective-permute-start) | collective-permute-done | bytes 1048608 | tf_op jit(solution)/shard_map/ppermute | solution.py:66
  27.7 0.1 select_bitcast_fusion.1
  27.9 1.5 %pad_maximum_fusion = bf16[8,2,256,256]{3,2,1,0:T(8,128)(2,1)} fusion(bf16[8,1,256,256]{3,2,1,0:T(8,128)(2,1)S(1)} %get-tuple-element.6, bf16[8,1,256,256]{3,2,1,0:T(8,128)(2,1)S(1)} %get-tuple-element.5), kind=kLoop, calls=%fused_computation | loop fusion | flops 1048576 | bytes 4194304 | tf_op jit(solution)/shard_map/stack | solution.py:69
  29.4 11.4 %shard_map.65 = f32[16,128,256]{2,1,0:T(8,128)} custom-call(s32[1]{0:T(128)} %bitcast.core_ref, s32[64]{0:T(128)} %bitcast_add_fusion.src_ref, s32[64]{0:T(128)} %tgt_ref.3, bf16[16,256,256]{2,1,0:T(8,128)(2,1)} %bitcast.17, bf16[64,4,2,32,256]{4,3,2,1,0:T(8,128)(2,1)} %bitcast.15, bf16[64,256,256]{2,1,0:T(8,128)(2,1)} %right_ref.3), custom_call_target="tpu_custom_call" | custom-call | tf_op jit(solution)/shard_map/pallas_call | solution.py:48
  40.8 0.1 collective-permute-start.1
  40.9 11.4 %shard_map.64 = f32[16,128,256]{2,1,0:T(8,128)} custom-call(s32[1]{0:T(128)} %bitcast.core_ref, s32[64]{0:T(128)} %bitcast_add_fusion.src_ref, s32[64]{0:T(128)} %tgt_ref.3, bf16[16,256,256]{2,1,0:T(8,128)(2,1)} %bitcast.18, bf16[64,4,2,32,256]{4,3,2,1,0:T(8,128)(2,1)} %bitcast.16, bf16[64,256,256]{2,1,0:T(8,128)(2,1)} %right_ref.3), custom_call_target="tpu_custom_call" | custom-call | tf_op jit(solution)/shard_map/pallas_call | solution.py:48
  52.3 0.0 collective-permute-done.1
  52.3 2.0 %add.12 = f32[64,32,256]{2,1,0:T(8,128)S(1)} add(f32[64,32,256]{2,1,0:T(8,128)} %bitcast.19, f32[64,32,256]{2,1,0:T(8,128)S(1)} %collective-permute-done.1) | non-fusion elementwise | flops 524288 | bytes 6291456 | tf_op jit(solution)/shard_map/add | solution.py:87
  54.3 37.2 %all_to_all.11 = f32[64,32,256]{2,1,0:T(8,128)S(1)} all-to-all(f32[64,32,256]{2,1,0:T(8,128)S(1)} %add.12), channel_id=1, replica_groups=mesh['y'=4,'xh'=2,'z'=4,'xl'=2,'c'=2] {'y','xh','z','xl'}, dimensions={0} | all-to-all | bytes 4194304 | tf_op jit(solution)/shard_map/all_to_all | solution.py:88
  91.5 0.8 reduce_sum.9
  (1 shorter events, 0.0 us)
Async XLA Ops:
  0.0 1.0 %copy-start = (bf16[2,256,256]{2,1,0:T(8,128)(2,1)S(1)}, bf16[2,256,256]{2,1,0:T(8,128)(2,1)}, u32[]{:S(2)}) copy-start(bf16[2,256,256]{2,1,0:T(8,128)(2,1)} %param.6) | copy-start | bytes 786436
  0.0 25.1 %copy-start.1 = (s32[64]{0:T(128)S(1)}, s32[64]{0:T(128)}, u32[]{:S(2)}) copy-start(s32[64]{0:T(128)} %param.10) | copy-start | bytes 772
  0.0 25.1 %copy-start.2 = (s32[64,1]{0,1:T(1,128)S(1)}, s32[64,1]{0,1:T(1,128)}, u32[]{:S(2)}) copy-start(s32[64,1]{0,1:T(1,128)} %param.9) | copy-start | bytes 772
  25.1 2.7 %collective-permute-start = (bf16[8,256,256]{2,1,0:T(8,128)(2,1)S(1)}, bf16[8,256,256]{2,1,0:T(8,128)(2,1)S(1)}, u32[]{:S(2)}, u32[]{:S(2)}) collective-permute-start(bf16[8,256,256]{2,1,0:T(8,128)(2,1)S(1)} %all_to_all.10), channel_id=1, source_target_pairs={{0,1},{1,0},{2,3},{3,2},{4,5},{5,4},{6,7},{7,6},{8,9},{9,8},{10,11... | collective-permute-start | bytes 3145736 | tf_op jit(solution)/shard_map/ppermute | solution.py:66
  40.8 11.5 %collective-permute-start.1 = (f32[64,32,256]{2,1,0:T(8,128)}, f32[64,32,256]{2,1,0:T(8,128)S(1)}, u32[]{:S(2)}, u32[]{:S(2)}) collective-permute-start(f32[64,32,256]{2,1,0:T(8,128)} %bitcast.20), channel_id=1, source_target_pairs={{0,1},{1,0},{2,3},{3,2},{4,5},{5,4},{6,7},{7,6},{8,9},{9,8},{10,11... | collective-permute-start | bytes 6291464 | tf_op jit(solution)/shard_map/ppermute | solution.py:85

commit v7 on v5

--- a/solution.py
+++ b/solution.py
@@ -10,11 +10,16 @@
 TERM_BLOCK = 32
 
 
-def sigma_kernel(src_ref, tgt_ref, psi_ref, left_ref, right_ref, out_ref):
+def sigma_kernel(core_ref, src_ref, tgt_ref, own_ref, swapped_ref, left_ref, right_ref,
+                 out_ref, psi_ref):
     step = pl.program_id(0)
 
     @pl.when(step == 0)
     def _():
+        core = core_ref[0]
+        for b in range(own_ref.shape[0]):
+            psi_ref[2 * b + core] = own_ref[b]
+            psi_ref[2 * b + 1 - core] = swapped_ref[b]
         out_ref[...] = jnp.zeros_like(out_ref)
 
     for j in range(TERM_BLOCK):
@@ -29,33 +34,34 @@
         out_ref[tgt_ref[t]] += term_image
 
 
-def add_terms(wave_blocks, left_terms, right_terms, sources, targets):
-    sectors, width, _ = wave_blocks.shape
+def add_terms(own, swapped, left_terms, right_terms, sources, targets, core):
+    n_slab, width, _ = own.shape
+    sectors = 2 * n_slab
     n_terms = left_terms.shape[0]
-    whole = pl.BlockSpec((sectors, width, width), lambda i, s, g: (0, 0, 0))
-    per_step = pl.BlockSpec((TERM_BLOCK, width, width), lambda i, s, g: (i, 0, 0))
+    half = pl.BlockSpec((n_slab, width, width), lambda i, *_: (0, 0, 0))
+    whole = pl.BlockSpec((sectors, width, width), lambda i, *_: (0, 0, 0))
+    per_step = pl.BlockSpec((TERM_BLOCK, width, width), lambda i, *_: (i, 0, 0))
     return pl.pallas_call(
         sigma_kernel,
         out_shape=jax.ShapeDtypeStruct((sectors, width, width), jnp.float32),
         grid_spec=pltpu.PrefetchScalarGridSpec(
-            num_scalar_prefetch=2,
+            num_scalar_prefetch=3,
             grid=(n_terms // TERM_BLOCK,),
-            in_specs=[whole, per_step, per_step],
+            in_specs=[half, half, per_step, per_step],
             out_specs=whole,
+            scratch_shapes=[pltpu.VMEM((sectors, width, width), own.dtype)],
         ),
         compiler_params=pltpu.CompilerParams(dimension_semantics=("arbitrary",)),
-    )(sources, targets, wave_blocks, left_terms, right_terms)
+    )(core, sources, targets, own, swapped, left_terms, right_terms)
 
 
 def gather_blocks(wavefunction, n_blk):
     core = lax.axis_index("c")
     mine = lax.dynamic_index_in_dim(wavefunction, core, 0, keepdims=False)
     copies = jnp.broadcast_to(mine[None], (n_blk,) + mine.shape)
-    got = lax.all_to_all(copies, ("y", "xh"), 0, 0, tiled=True)
-    other = lax.ppermute(got, "c", [(0, 1), (1, 0)])
-    low = jnp.where(core == 0, got, other)
-    high = jnp.where(core == 0, other, got)
-    return jnp.stack([low, high], 1).reshape((-1,) + wavefunction.shape[1:])
+    own = lax.all_to_all(copies, ("y", "xh"), 0, 0, tiled=True)
+    swapped = lax.ppermute(own, "c", [(0, 1), (1, 0)])
+    return own, swapped
 
 
 def reduce_rows(stacked, n_core, n_rest):
@@ -77,8 +83,9 @@
     sectors = per_slab * n_blk
     block_width = wavefunction.shape[1]
     sources = term_slab[:, 0] * per_slab + term_sector
-    gathered = gather_blocks(wavefunction, n_blk)
-    partial_value = add_terms(gathered, left_terms, right_terms, sources, term_target)
+    core = lax.axis_index("c").astype(jnp.int32).reshape(1)
+    own, swapped = gather_blocks(wavefunction, n_blk)
+    partial_value = add_terms(own, swapped, left_terms, right_terms, sources, term_target, core)
     stacked = partial_value.reshape(sectors * block_width, block_width)
     return reduce_rows(stacked, n_core, n_rest)
 

time: 87.3 us -> 86.7 us (level)
  other arithmetic: 6.62 us -> 5.09 us
  local copies, waits for them, and re-layouts: 1.04 us -> 2.04 us
    another operation x2 -> x0, other arithmetic: 1.65 us -> none  [gather_blocks(): return jnp.stack([low, high], 1).reshape((-1,) + wavefunction.shape[1:])]
    unnamed x8 -> x12, local copies, waits for them, and re-layouts: 0.96 us -> 1.96 us
where the time goes in v7:
time: 86.7 us; the launch traced here: 86.5 us
  blocking collectives  61.2 us (71%)
  Pallas kernels  11.9 us (14%)
  waiting for transfers between devices  6.03 us (7%)
  other arithmetic  5.09 us (6%)
  local copies, waits for them, and re-layouts  2.04 us (2%)
    all_to_all x1, blocking collectives, reduce_rows(): y = lax.all_to_all(y, ('y', 'xh', 'z', 'xl'), 0, 0, tiled=True)  37.1 us
    all_to_all x1, blocking collectives, gather_blocks(): own = lax.all_to_all(copies, ('y', 'xh'), 0, 0, tiled=True)  24 us
    pallas_call x1, Pallas kernels, add_terms(): pl.pallas_call(sigma_kernel, out_shape=jax.ShapeDtypeStruct((sectors, wid...  11.9 us
    ppermute x1, waiting for transfers between devices, reduce_rows(): y = mine + lax.ppermute(other, 'c', [(0, 1), (1, 0)])  4.02 us
    select_n x1, other arithmetic, reduce_rows(): other = jnp.where(core == 0, y[:, 1], y[:, 0])  2.84 us
    ppermute x1, waiting for transfers between devices, gather_blocks(): swapped = lax.ppermute(own, 'c', [(0, 1), (1, 0)])  2.01 us
    unnamed x12, local copies, waits for them, and re-layouts  1.96 us
  transfers between devices with their start and end apart: 2, of which 2 were waited for; matrix products, arithmetic and copies ran while one was open for 1% of the time, Pallas kernels for 0%

profile of v7, /device:TPU:0, one launch (start us, length us, event | category | flops | bytes accessed | tf_op | source)
XLA Modules:
  0.0 86.5 jit_solution(14449556047016482616)
XLA Ops:
  0.0 0.0 copy-start
  0.0 0.0 copy-start.4
  0.0 0.0 copy-start.5
  0.0 0.9 %copy-done = bf16[2,256,256]{2,1,0:T(8,128)(2,1)S(1)} copy-done((bf16[2,256,256]{2,1,0:T(8,128)(2,1)S(1)}, bf16[2,256,256]{2,1,0:T(8,128)(2,1)}, u32[]{:S(2)}) %copy-start) | copy-done | bytes 262168
  1.0 0.1 broadcast_in_dim.9
  1.0 24.0 %all_to_all.10.own_ref = bf16[8,256,256]{2,1,0:T(8,128)(2,1)S(1)} all-to-all(bf16[8,256,256]{2,1,0:T(8,128)(2,1)S(1)} %broadcast_in_dim.9), channel_id=1, replica_groups=mesh['y'=4,'xh'=2,'z'=4,'xl'=2,'c'=2] {'y','xh'}, dimensions={0} | all-to-all | bytes 2097152 | tf_op jit(solution)/shard_map/all_to_all | solution.py:62
  25.1 0.0 copy-start.2
  25.1 0.0 collective-permute-start
  25.1 0.0 copy-done.4
  25.1 0.0 copy-done.5
  25.1 0.6 bitcast_add_fusion.src_ref
  25.7 2.0 %collective-permute-done.swapped_ref = bf16[8,256,256]{2,1,0:T(8,128)(2,1)S(1)} collective-permute-done((bf16[8,256,256]{2,1,0:T(8,128)(2,1)S(1)}, bf16[8,256,256]{2,1,0:T(8,128)(2,1)S(1)}, u32[]{:S(2)}, u32[]{:S(2)}) %collective-permute-start) | collective-permute-done | bytes 1048608 | tf_op jit(solution)/shard_map/ppermute | solution.py:63
  27.7 0.0 copy-start.3
  27.7 0.0 copy-done.2
  27.8 1.0 %copy-done.3 = bf16[8,256,256]{2,1,0:T(8,128)(2,1)} copy-done((bf16[8,256,256]{2,1,0:T(8,128)(2,1)}, bf16[8,256,256]{2,1,0:T(8,128)(2,1)S(1)}, u32[]{:S(2)}) %copy-start.3) | copy-done | bytes 1048600
  28.8 11.9 %shard_map.64 = f32[16,256,256]{2,1,0:T(8,128)} custom-call(s32[1]{0:T(128)} %bitcast.core_ref, s32[64]{0:T(128)} %bitcast_add_fusion.src_ref, s32[64]{0:T(128)} %tgt_ref.1, bf16[8,256,256]{2,1,0:T(8,128)(2,1)} %copy-done.2, bf16[8,256,256]{2,1,0:T(8,128)(2,1)} %copy-done.3, bf16[64,256,256]{2,1,0:T(8,128)(2,1)} %left_ref.1, bf16[64,256,256]{2,1,0:T(8,128)(2,1)} %right_ref.1), custom_call_target="tpu_custom_call" | custom-call | tf_op jit(solution)/shard_map/pallas_call | solution.py:44
  40.7 0.0 copy-start.1
  40.7 2.8 %select_bitcast_fusion = f32[64,32,256]{2,1,0:T(8,128)S(1)} fusion(f32[64,2,32,256]{3,2,1,0:T(8,128)} %bitcast.24, pred[]{:T(512)S(6)} %eq.4), kind=kLoop, calls=%fused_computation.3 | loop fusion | flops 524288 | bytes 6291457 | tf_op jit(solution)/shard_map/jit(_where)/select_n | solution.py:72
  43.6 0.2 collective-permute-start.1
  43.8 4.0 %collective-permute-done.1 = f32[64,32,256]{2,1,0:T(8,128)S(1)} collective-permute-done((f32[64,32,256]{2,1,0:T(8,128)S(1)}, f32[64,32,256]{2,1,0:T(8,128)S(1)}, u32[]{:S(2)}, u32[]{:S(2)}) %collective-permute-start.1) | collective-permute-done | bytes 2097184 | tf_op jit(solution)/shard_map/ppermute | solution.py:73
  47.8 0.0 copy-done.1
  47.8 0.9 fusion.1
  48.7 37.1 %all_to_all.11 = f32[64,32,256]{2,1,0:T(8,128)S(1)} all-to-all(f32[64,32,256]{2,1,0:T(8,128)S(1)} %fusion.1), channel_id=1, replica_groups=mesh['y'=4,'xh'=2,'z'=4,'xl'=2,'c'=2] {'y','xh','z','xl'}, dimensions={0} | all-to-all | bytes 4194304 | tf_op jit(solution)/shard_map/all_to_all | solution.py:74
  85.8 0.8 reduce_sum.9
  (1 shorter events, 0.0 us)
Async XLA Ops:
  0.0 1.0 %copy-start = (bf16[2,256,256]{2,1,0:T(8,128)(2,1)S(1)}, bf16[2,256,256]{2,1,0:T(8,128)(2,1)}, u32[]{:S(2)}) copy-start(bf16[2,256,256]{2,1,0:T(8,128)(2,1)} %param.6) | copy-start | bytes 786436
  0.0 25.1 %copy-start.4 = (s32[64]{0:T(128)S(1)}, s32[64]{0:T(128)}, u32[]{:S(2)}) copy-start(s32[64]{0:T(128)} %param.10) | copy-start | bytes 772
  0.0 25.1 %copy-start.5 = (s32[64,1]{0,1:T(1,128)S(1)}, s32[64,1]{0,1:T(1,128)}, u32[]{:S(2)}) copy-start(s32[64,1]{0,1:T(1,128)} %param.9) | copy-start | bytes 772
  25.1 2.7 %copy-start.2 = (bf16[8,256,256]{2,1,0:T(8,128)(2,1)}, bf16[8,256,256]{2,1,0:T(8,128)(2,1)S(1)}, u32[]{:S(2)}) copy-start(bf16[8,256,256]{2,1,0:T(8,128)(2,1)S(1)} %all_to_all.10.own_ref) | copy-start | bytes 3145732
  25.1 2.7 %collective-permute-start = (bf16[8,256,256]{2,1,0:T(8,128)(2,1)S(1)}, bf16[8,256,256]{2,1,0:T(8,128)(2,1)S(1)}, u32[]{:S(2)}, u32[]{:S(2)}) collective-permute-start(bf16[8,256,256]{2,1,0:T(8,128)(2,1)S(1)} %all_to_all.10.own_ref), channel_id=1, source_target_pairs={{0,1},{1,0},{2,3},{3,2},{4,5},{5,4},{6,7},{7,6},{8,9},{9,8},{10,11... | collective-permute-start | bytes 3145736 | tf_op jit(solution)/shard_map/ppermute | solution.py:63
  27.7 1.0 %copy-start.3 = (bf16[8,256,256]{2,1,0:T(8,128)(2,1)}, bf16[8,256,256]{2,1,0:T(8,128)(2,1)S(1)}, u32[]{:S(2)}) copy-start(bf16[8,256,256]{2,1,0:T(8,128)(2,1)S(1)} %collective-permute-done.swapped_ref) | copy-start | bytes 3145732
  40.7 7.1 %copy-start.1 = (f32[16,256,256]{2,1,0:T(8,128)S(1)}, f32[16,256,256]{2,1,0:T(8,128)}, u32[]{:S(2)}) copy-start(f32[16,256,256]{2,1,0:T(8,128)} %shard_map.64) | copy-start | bytes 12582916
  43.6 4.2 %collective-permute-start.1 = (f32[64,32,256]{2,1,0:T(8,128)S(1)}, f32[64,32,256]{2,1,0:T(8,128)S(1)}, u32[]{:S(2)}, u32[]{:S(2)}) collective-permute-start(f32[64,32,256]{2,1,0:T(8,128)S(1)} %select_bitcast_fusion), channel_id=1, source_target_pairs={{0,1},{1,0},{2,3},{3,2},{4,5},{5,4},{6,7},{7,6},{8,9},{9,8},{10,11... | collective-permute-start | bytes 6291464 | tf_op jit(solution)/shard_map/ppermute | solution.py:73

commit v8 on v7

--- a/solution.py
+++ b/solution.py
@@ -31,19 +31,25 @@
             left_part, right_ref[j], (((1,), (1,)), ((), ())),
             preferred_element_type=jnp.float32,
         )
-        out_ref[tgt_ref[t]] += term_image
+        n_core, _, bands, band, _ = out_ref.shape
+        target = tgt_ref[t]
+        for q in range(bands):
+            for cc in range(n_core):
+                row = (q * n_core + cc) * band
+                out_ref[cc, target, q] += term_image[row:row + band]
 
 
-def add_terms(own, swapped, left_terms, right_terms, sources, targets, core):
+def add_terms(own, swapped, left_terms, right_terms, sources, targets, core, n_core, band):
     n_slab, width, _ = own.shape
     sectors = 2 * n_slab
     n_terms = left_terms.shape[0]
+    out_shape = (n_core, sectors, width // (n_core * band), band, width)
     half = pl.BlockSpec((n_slab, width, width), lambda i, *_: (0, 0, 0))
-    whole = pl.BlockSpec((sectors, width, width), lambda i, *_: (0, 0, 0))
+    whole = pl.BlockSpec(out_shape, lambda i, *_: (0,) * len(out_shape))
     per_step = pl.BlockSpec((TERM_BLOCK, width, width), lambda i, *_: (i, 0, 0))
     return pl.pallas_call(
         sigma_kernel,
-        out_shape=jax.ShapeDtypeStruct((sectors, width, width), jnp.float32),
+        out_shape=jax.ShapeDtypeStruct(out_shape, jnp.float32),
         grid_spec=pltpu.PrefetchScalarGridSpec(
             num_scalar_prefetch=3,
             grid=(n_terms // TERM_BLOCK,),
@@ -64,30 +70,22 @@
     return own, swapped
 
 
-def reduce_rows(stacked, n_core, n_rest):
-    rows = stacked.shape[0] // (n_core * n_rest)
-    y = stacked.reshape(n_rest, n_core, rows, stacked.shape[1])
-    core = lax.axis_index("c")
-    mine = jnp.where(core == 0, y[:, 0], y[:, 1])
-    other = jnp.where(core == 0, y[:, 1], y[:, 0])
-    y = mine + lax.ppermute(other, "c", [(0, 1), (1, 0)])
-    y = lax.all_to_all(y, ("y", "xh", "z", "xl"), 0, 0, tiled=True)
-    return y.sum(0)
-
-
 def on_device(wavefunction, left_terms, right_terms, term_slab, term_sector, term_target):
     per_slab = wavefunction.shape[0]
     n_blk = lax.axis_size(("y", "xh"))
     n_core = lax.axis_size("c")
     n_rest = lax.axis_size(("y", "xh", "z", "xl"))
-    sectors = per_slab * n_blk
-    block_width = wavefunction.shape[1]
+    width = wavefunction.shape[1]
+    band = per_slab * n_blk * width // (n_core * n_rest)
     sources = term_slab[:, 0] * per_slab + term_sector
     core = lax.axis_index("c").astype(jnp.int32).reshape(1)
     own, swapped = gather_blocks(wavefunction, n_blk)
-    partial_value = add_terms(own, swapped, left_terms, right_terms, sources, term_target, core)
-    stacked = partial_value.reshape(sectors * block_width, block_width)
-    return reduce_rows(stacked, n_core, n_rest)
+    parts = add_terms(own, swapped, left_terms, right_terms, sources, term_target, core, n_core, band)
+    mine = lax.dynamic_index_in_dim(parts, core[0], 0, keepdims=False).reshape(n_rest, band, width)
+    other = lax.dynamic_index_in_dim(parts, 1 - core[0], 0, keepdims=False).reshape(n_rest, band, width)
+    summed = mine + lax.ppermute(other, "c", [(0, 1), (1, 0)])
+    got = lax.all_to_all(summed, ("y", "xh", "z", "xl"), 0, 0, tiled=True)
+    return got.sum(0)
 
 
 def solution(mesh):

time: 86.7 us -> 86.1 us (level)
  other arithmetic: 5.09 us -> 1.87 us
  local copies, waits for them, and re-layouts: 2.04 us -> 4.58 us
    select_n x1 -> x0, other arithmetic: 2.84 us -> none  [reduce_rows(): other = jnp.where(core == 0, y[:, 1], y[:, 0])]
    dynamic_slice x0 -> x1, local copies, waits for them, and re-layouts: none -> 2.54 us  [on_device(): lax.dynamic_index_in_dim(parts, core[0], 0, keepdims=False)]
    unnamed x12 -> x10, local copies, waits for them, and re-layouts: 1.96 us -> 1.96 us
where the time goes in v8:
time: 86.1 us; the launch traced here: 85.9 us
  blocking collectives  61.2 us (71%)
  Pallas kernels  11.9 us (14%)
  waiting for transfers between devices  6.03 us (7%)
  local copies, waits for them, and re-layouts  4.58 us (5%)
  other arithmetic  1.87 us (2%)
    all_to_all x1, blocking collectives, on_device(): got = lax.all_to_all(summed, ('y', 'xh', 'z', 'xl'), 0, 0, tiled=True)  37.1 us
    all_to_all x1, blocking collectives, gather_blocks(): own = lax.all_to_all(copies, ('y', 'xh'), 0, 0, tiled=True)  24 us
    pallas_call x1, Pallas kernels, add_terms(): pl.pallas_call(sigma_kernel, out_shape=jax.ShapeDtypeStruct(out_shape, jn...  11.9 us
    ppermute x1, waiting for transfers between devices, on_device(): summed = mine + lax.ppermute(other, 'c', [(0, 1), (1, 0)])  4.02 us
    dynamic_slice x1, local copies, waits for them, and re-layouts, on_device(): lax.dynamic_index_in_dim(parts, core[0], 0, keepdims=False)  2.54 us
    ppermute x1, waiting for transfers between devices, gather_blocks(): swapped = lax.ppermute(own, 'c', [(0, 1), (1, 0)])  2.01 us
    unnamed x10, local copies, waits for them, and re-layouts  1.96 us
  transfers between devices with their start and end apart: 2, of which 2 were waited for; matrix products, arithmetic and copies ran while one was open for 1% of the time, Pallas kernels for 0%

profile of v8, /device:TPU:0, one launch (start us, length us, event | category | flops | bytes accessed | tf_op | source)
XLA Modules:
  0.0 85.9 jit_solution(17398741262135071174)
XLA Ops:
  0.0 0.0 copy-start
  0.0 0.0 copy-start.3
  0.0 0.0 copy-start.4
  0.0 0.9 %copy-done = bf16[2,256,256]{2,1,0:T(8,128)(2,1)S(1)} copy-done((bf16[2,256,256]{2,1,0:T(8,128)(2,1)S(1)}, bf16[2,256,256]{2,1,0:T(8,128)(2,1)}, u32[]{:S(2)}) %copy-start) | copy-done | bytes 262168
  1.0 0.1 broadcast_in_dim.9
  1.0 24.0 %all_to_all.10.own_ref = bf16[8,256,256]{2,1,0:T(8,128)(2,1)S(1)} all-to-all(bf16[8,256,256]{2,1,0:T(8,128)(2,1)S(1)} %broadcast_in_dim.9), channel_id=1, replica_groups=mesh['y'=4,'xh'=2,'z'=4,'xl'=2,'c'=2] {'y','xh'}, dimensions={0} | all-to-all | bytes 2097152 | tf_op jit(solution)/shard_map/all_to_all | solution.py:68
  25.1 0.0 copy-start.1
  25.1 0.0 collective-permute-start
  25.1 0.0 copy-done.3
  25.1 0.0 copy-done.4
  25.1 0.6 bitcast_add_fusion.1.src_ref
  25.7 2.0 %collective-permute-done.swapped_ref = bf16[8,256,256]{2,1,0:T(8,128)(2,1)S(1)} collective-permute-done((bf16[8,256,256]{2,1,0:T(8,128)(2,1)S(1)}, bf16[8,256,256]{2,1,0:T(8,128)(2,1)S(1)}, u32[]{:S(2)}, u32[]{:S(2)}) %collective-permute-start) | collective-permute-done | bytes 1048608 | tf_op jit(solution)/shard_map/ppermute | solution.py:69
  27.7 0.0 copy-start.2
  27.7 0.0 copy-done.1
  27.8 1.0 %copy-done.2 = bf16[8,256,256]{2,1,0:T(8,128)(2,1)} copy-done((bf16[8,256,256]{2,1,0:T(8,128)(2,1)}, bf16[8,256,256]{2,1,0:T(8,128)(2,1)S(1)}, u32[]{:S(2)}) %copy-start.2) | copy-done | bytes 1048600
  28.8 11.9 %shard_map.64 = f32[2,16,4,32,256]{4,3,2,1,0:T(8,128)} custom-call(s32[1]{0:T(128)} %bitcast.core_ref, s32[64]{0:T(128)} %bitcast_add_fusion.1.src_ref, s32[64]{0:T(128)} %tgt_ref.1, bf16[8,256,256]{2,1,0:T(8,128)(2,1)} %copy-done.1, bf16[8,256,256]{2,1,0:T(8,128)(2,1)} %copy-done.2, bf16[64,256,256]{2,1,0:T(8,128)(2,1)} %left_ref.1, ...), custom_call_target="tpu_custom_call" | custom-call | tf_op jit(solution)/shard_map/pallas_call | solution.py:50
  40.7 2.5 %constant_dynamic-slice_fusion.1 = (f32[1,16,4,32,256]{4,3,2,1,0:T(8,128)S(1)}, f32[1,16,4,32,256]{4,3,2,1,0:T(8,128)S(1)}) fusion(f32[2,16,4,32,256]{4,3,2,1,0:T(8,128)} %shard_map.64, s32[]{:T(128)S(6)} %select_n.9, s32[]{:T(128)S(6)} %select_n.10), kind=kLoop, calls=%fused_computation.3 | loop fusion | bytes 8388616 | tf_op jit(solution)/shard_map/jit(dynamic_index_in_dim)/dynamic_slice | solution.py:84
  43.2 0.2 collective-permute-start.1
  43.5 4.0 %collective-permute-done.1 = f32[64,32,256]{2,1,0:T(8,128)S(1)} collective-permute-done((f32[64,32,256]{2,1,0:T(8,128)S(1)}, f32[64,32,256]{2,1,0:T(8,128)S(1)}, u32[]{:S(2)}, u32[]{:S(2)}) %collective-permute-start.1) | collective-permute-done | bytes 2097184 | tf_op jit(solution)/shard_map/ppermute | solution.py:86
  47.5 0.5 bitcast_add_fusion
  48.0 37.1 %all_to_all.11 = f32[64,32,256]{2,1,0:T(8,128)S(1)} all-to-all(f32[64,32,256]{2,1,0:T(8,128)S(1)} %bitcast_add_fusion), channel_id=1, replica_groups=mesh['y'=4,'xh'=2,'z'=4,'xl'=2,'c'=2] {'y','xh','z','xl'}, dimensions={0} | all-to-all | bytes 4194304 | tf_op jit(solution)/shard_map/all_to_all | solution.py:87
  85.1 0.8 reduce_sum.9
  (1 shorter events, 0.0 us)
Async XLA Ops:
  0.0 1.0 %copy-start = (bf16[2,256,256]{2,1,0:T(8,128)(2,1)S(1)}, bf16[2,256,256]{2,1,0:T(8,128)(2,1)}, u32[]{:S(2)}) copy-start(bf16[2,256,256]{2,1,0:T(8,128)(2,1)} %param.6) | copy-start | bytes 786436
  0.0 25.1 %copy-start.3 = (s32[64]{0:T(128)S(1)}, s32[64]{0:T(128)}, u32[]{:S(2)}) copy-start(s32[64]{0:T(128)} %param.10) | copy-start | bytes 772
  0.0 25.1 %copy-start.4 = (s32[64,1]{0,1:T(1,128)S(1)}, s32[64,1]{0,1:T(1,128)}, u32[]{:S(2)}) copy-start(s32[64,1]{0,1:T(1,128)} %param.9) | copy-start | bytes 772
  25.1 2.7 %copy-start.1 = (bf16[8,256,256]{2,1,0:T(8,128)(2,1)}, bf16[8,256,256]{2,1,0:T(8,128)(2,1)S(1)}, u32[]{:S(2)}) copy-start(bf16[8,256,256]{2,1,0:T(8,128)(2,1)S(1)} %all_to_all.10.own_ref) | copy-start | bytes 3145732
  25.1 2.7 %collective-permute-start = (bf16[8,256,256]{2,1,0:T(8,128)(2,1)S(1)}, bf16[8,256,256]{2,1,0:T(8,128)(2,1)S(1)}, u32[]{:S(2)}, u32[]{:S(2)}) collective-permute-start(bf16[8,256,256]{2,1,0:T(8,128)(2,1)S(1)} %all_to_all.10.own_ref), channel_id=1, source_target_pairs={{0,1},{1,0},{2,3},{3,2},{4,5},{5,4},{6,7},{7,6},{8,9},{9,8},{10,11... | collective-permute-start | bytes 3145736 | tf_op jit(solution)/shard_map/ppermute | solution.py:69
  27.7 1.0 %copy-start.2 = (bf16[8,256,256]{2,1,0:T(8,128)(2,1)}, bf16[8,256,256]{2,1,0:T(8,128)(2,1)S(1)}, u32[]{:S(2)}) copy-start(bf16[8,256,256]{2,1,0:T(8,128)(2,1)S(1)} %collective-permute-done.swapped_ref) | copy-start | bytes 3145732
  43.2 4.2 %collective-permute-start.1 = (f32[64,32,256]{2,1,0:T(8,128)S(1)}, f32[64,32,256]{2,1,0:T(8,128)S(1)}, u32[]{:S(2)}, u32[]{:S(2)}) collective-permute-start(f32[64,32,256]{2,1,0:T(8,128)S(1)} %bitcast.8), channel_id=1, source_target_pairs={{0,1},{1,0},{2,3},{3,2},{4,5},{5,4},{6,7},{7,6},{8,9},{9,8},{10,11... | collective-permute-start | bytes 6291464 | tf_op jit(solution)/shard_map/ppermute | solution.py:86

commit v9 on v8

--- a/solution.py
+++ b/solution.py
@@ -11,7 +11,7 @@
 
 
 def sigma_kernel(core_ref, src_ref, tgt_ref, own_ref, swapped_ref, left_ref, right_ref,
-                 out_ref, psi_ref):
+                 mine_ref, other_ref, psi_ref):
     step = pl.program_id(0)
 
     @pl.when(step == 0)
@@ -20,7 +20,8 @@
         for b in range(own_ref.shape[0]):
             psi_ref[2 * b + core] = own_ref[b]
             psi_ref[2 * b + 1 - core] = swapped_ref[b]
-        out_ref[...] = jnp.zeros_like(out_ref)
+        mine_ref[...] = jnp.zeros_like(mine_ref)
+        other_ref[...] = jnp.zeros_like(other_ref)
 
     for j in range(TERM_BLOCK):
         t = step * TERM_BLOCK + j
@@ -31,30 +32,32 @@
             left_part, right_ref[j], (((1,), (1,)), ((), ())),
             preferred_element_type=jnp.float32,
         )
-        n_core, _, bands, band, _ = out_ref.shape
+        _, bands, band, _ = mine_ref.shape
         target = tgt_ref[t]
+        first = core_ref[0] == 0
         for q in range(bands):
-            for cc in range(n_core):
-                row = (q * n_core + cc) * band
-                out_ref[cc, target, q] += term_image[row:row + band]
+            low = term_image[2 * q * band:(2 * q + 1) * band]
+            high = term_image[(2 * q + 1) * band:(2 * q + 2) * band]
+            mine_ref[target, q] += jnp.where(first, low, high)
+            other_ref[target, q] += jnp.where(first, high, low)
 
 
 def add_terms(own, swapped, left_terms, right_terms, sources, targets, core, n_core, band):
     n_slab, width, _ = own.shape
     sectors = 2 * n_slab
     n_terms = left_terms.shape[0]
-    out_shape = (n_core, sectors, width // (n_core * band), band, width)
+    out_shape = (sectors, width // (n_core * band), band, width)
     half = pl.BlockSpec((n_slab, width, width), lambda i, *_: (0, 0, 0))
     whole = pl.BlockSpec(out_shape, lambda i, *_: (0,) * len(out_shape))
     per_step = pl.BlockSpec((TERM_BLOCK, width, width), lambda i, *_: (i, 0, 0))
     return pl.pallas_call(
         sigma_kernel,
-        out_shape=jax.ShapeDtypeStruct(out_shape, jnp.float32),
+        out_shape=(jax.ShapeDtypeStruct(out_shape, jnp.float32),) * 2,
         grid_spec=pltpu.PrefetchScalarGridSpec(
             num_scalar_prefetch=3,
             grid=(n_terms // TERM_BLOCK,),
             in_specs=[half, half, per_step, per_step],
-            out_specs=whole,
+            out_specs=(whole, whole),
             scratch_shapes=[pltpu.VMEM((sectors, width, width), own.dtype)],
         ),
         compiler_params=pltpu.CompilerParams(dimension_semantics=("arbitrary",)),
@@ -80,9 +83,9 @@
     sources = term_slab[:, 0] * per_slab + term_sector
     core = lax.axis_index("c").astype(jnp.int32).reshape(1)
     own, swapped = gather_blocks(wavefunction, n_blk)
-    parts = add_terms(own, swapped, left_terms, right_terms, sources, term_target, core, n_core, band)
-    mine = lax.dynamic_index_in_dim(parts, core[0], 0, keepdims=False).reshape(n_rest, band, width)
-    other = lax.dynamic_index_in_dim(parts, 1 - core[0], 0, keepdims=False).reshape(n_rest, band, width)
+    mine, other = add_terms(own, swapped, left_terms, right_terms, sources, term_target, core, n_core, band)
+    mine = mine.reshape(n_rest, band, width)
+    other = other.reshape(n_rest, band, width)
     summed = mine + lax.ppermute(other, "c", [(0, 1), (1, 0)])
     got = lax.all_to_all(summed, ("y", "xh", "z", "xl"), 0, 0, tiled=True)
     return got.sum(0)

time: 86.1 us -> 85.2 us (0.990)
  local copies, waits for them, and re-layouts: 4.58 us -> 2.04 us
  other arithmetic: 1.87 us -> 3.41 us
    dynamic_slice x1 -> x0, local copies, waits for them, and re-layouts: 2.54 us -> none  [on_device(): lax.dynamic_index_in_dim(parts, core[0], 0, keepdims=False)]
    add x1, other arithmetic: 0.49 us -> 2.03 us  [on_device(): summed = mine + lax.ppermute(other, 'c', [(0, 1), (1, 0)])]
where the time goes in v9:
time: 85.2 us; the launch traced here: 85 us
  blocking collectives  61.2 us (72%)
  Pallas kernels  12 us (14%)
  waiting for transfers between devices  6.25 us (7%)
  other arithmetic  3.41 us (4%)
  local copies, waits for them, and re-layouts  2.04 us (2%)
    all_to_all x1, blocking collectives, on_device(): got = lax.all_to_all(summed, ('y', 'xh', 'z', 'xl'), 0, 0, tiled=True)  37.1 us
    all_to_all x1, blocking collectives, gather_blocks(): own = lax.all_to_all(copies, ('y', 'xh'), 0, 0, tiled=True)  24 us
    pallas_call x1, Pallas kernels, add_terms(): pl.pallas_call(sigma_kernel, out_shape=(jax.ShapeDtypeStruct(out_shape, j...  12 us
    ppermute x1, waiting for transfers between devices, on_device(): summed = mine + lax.ppermute(other, 'c', [(0, 1), (1, 0)])  4.24 us
    add x1, other arithmetic, on_device(): summed = mine + lax.ppermute(other, 'c', [(0, 1), (1, 0)])  2.03 us
    ppermute x1, waiting for transfers between devices, gather_blocks(): swapped = lax.ppermute(own, 'c', [(0, 1), (1, 0)])  2.01 us
    unnamed x10, local copies, waits for them, and re-layouts  1.96 us
  transfers between devices with their start and end apart: 2, of which 2 were waited for; matrix products, arithmetic and copies ran while one was open for 1% of the time, Pallas kernels for 0%

profile of v9, /device:TPU:0, one launch (start us, length us, event | category | flops | bytes accessed | tf_op | source)
XLA Modules:
  0.0 85.0 jit_solution(17680469858794984582)
XLA Ops:
  0.0 0.0 copy-start
  0.0 0.0 copy-start.3
  0.0 0.0 copy-start.4
  0.0 0.9 %copy-done = bf16[2,256,256]{2,1,0:T(8,128)(2,1)S(1)} copy-done((bf16[2,256,256]{2,1,0:T(8,128)(2,1)S(1)}, bf16[2,256,256]{2,1,0:T(8,128)(2,1)}, u32[]{:S(2)}) %copy-start) | copy-done | bytes 262168
  1.0 0.1 broadcast_in_dim.9
  1.0 24.0 %all_to_all.10.own_ref = bf16[8,256,256]{2,1,0:T(8,128)(2,1)S(1)} all-to-all(bf16[8,256,256]{2,1,0:T(8,128)(2,1)S(1)} %broadcast_in_dim.9), channel_id=1, replica_groups=mesh['y'=4,'xh'=2,'z'=4,'xl'=2,'c'=2] {'y','xh'}, dimensions={0} | all-to-all | bytes 2097152 | tf_op jit(solution)/shard_map/all_to_all | solution.py:71
  25.1 0.0 copy-start.1
  25.1 0.0 collective-permute-start
  25.1 0.0 copy-done.3
  25.1 0.0 copy-done.4
  25.1 0.6 bitcast_add_fusion.1.src_ref
  25.7 2.0 %collective-permute-done.swapped_ref = bf16[8,256,256]{2,1,0:T(8,128)(2,1)S(1)} collective-permute-done((bf16[8,256,256]{2,1,0:T(8,128)(2,1)S(1)}, bf16[8,256,256]{2,1,0:T(8,128)(2,1)S(1)}, u32[]{:S(2)}, u32[]{:S(2)}) %collective-permute-start) | collective-permute-done | bytes 1048608 | tf_op jit(solution)/shard_map/ppermute | solution.py:72
  27.7 0.0 copy-start.2
  27.7 0.0 copy-done.1
  27.8 1.0 %copy-done.2 = bf16[8,256,256]{2,1,0:T(8,128)(2,1)} copy-done((bf16[8,256,256]{2,1,0:T(8,128)(2,1)}, bf16[8,256,256]{2,1,0:T(8,128)(2,1)S(1)}, u32[]{:S(2)}) %copy-start.2) | copy-done | bytes 1048600
  28.8 12.0 %shard_map.64 = (f32[16,4,32,256]{3,2,1,0:T(8,128)}, f32[16,4,32,256]{3,2,1,0:T(8,128)}) custom-call(s32[1]{0:T(128)} %bitcast.core_ref, s32[64]{0:T(128)} %bitcast_add_fusion.1.src_ref, s32[64]{0:T(128)} %tgt_ref.1, bf16[8,256,256]{2,1,0:T(8,128)(2,1)} %copy-done.1, bf16[8,256,256]{2,1,0:T(8,128)(2,1)} %copy-done.2, bf16[64,256,256]{2,1,0:T(8,128)(2,1)} %left_ref.1, ...), custom_call_target="tpu_custom_call" | custom-call | tf_op jit(solution)/shard_map/pallas_call | solution.py:53
  40.7 0.1 collective-permute-start.1
  40.8 4.2 %collective-permute-done.1 = f32[64,32,256]{2,1,0:T(8,128)S(1)} collective-permute-done((f32[64,32,256]{2,1,0:T(8,128)}, f32[64,32,256]{2,1,0:T(8,128)S(1)}, u32[]{:S(2)}, u32[]{:S(2)}) %collective-permute-start.1) | collective-permute-done | bytes 2097184 | tf_op jit(solution)/shard_map/ppermute | solution.py:89
  45.1 2.0 %bitcast_add_fusion = f32[64,32,256]{2,1,0:T(8,128)S(1)} fusion(f32[64,32,256]{2,1,0:T(8,128)S(1)} %collective-permute-done.1, f32[16,4,32,256]{3,2,1,0:T(8,128)} %get-tuple-element.7), kind=kLoop, calls=%fused_computation | loop fusion | flops 524288 | bytes 6291456 | tf_op jit(solution)/shard_map/add | solution.py:89
  47.1 37.1 %all_to_all.11 = f32[64,32,256]{2,1,0:T(8,128)S(1)} all-to-all(f32[64,32,256]{2,1,0:T(8,128)S(1)} %bitcast_add_fusion), channel_id=1, replica_groups=mesh['y'=4,'xh'=2,'z'=4,'xl'=2,'c'=2] {'y','xh','z','xl'}, dimensions={0} | all-to-all | bytes 4194304 | tf_op jit(solution)/shard_map/all_to_all | solution.py:90
  84.2 0.8 reduce_sum.9
  (1 shorter events, 0.0 us)
Async XLA Ops:
  0.0 1.0 %copy-start = (bf16[2,256,256]{2,1,0:T(8,128)(2,1)S(1)}, bf16[2,256,256]{2,1,0:T(8,128)(2,1)}, u32[]{:S(2)}) copy-start(bf16[2,256,256]{2,1,0:T(8,128)(2,1)} %param.6) | copy-start | bytes 786436
  0.0 25.1 %copy-start.3 = (s32[64]{0:T(128)S(1)}, s32[64]{0:T(128)}, u32[]{:S(2)}) copy-start(s32[64]{0:T(128)} %param.10) | copy-start | bytes 772
  0.0 25.1 %copy-start.4 = (s32[64,1]{0,1:T(1,128)S(1)}, s32[64,1]{0,1:T(1,128)}, u32[]{:S(2)}) copy-start(s32[64,1]{0,1:T(1,128)} %param.9) | copy-start | bytes 772
  25.1 2.7 %copy-start.1 = (bf16[8,256,256]{2,1,0:T(8,128)(2,1)}, bf16[8,256,256]{2,1,0:T(8,128)(2,1)S(1)}, u32[]{:S(2)}) copy-start(bf16[8,256,256]{2,1,0:T(8,128)(2,1)S(1)} %all_to_all.10.own_ref) | copy-start | bytes 3145732
  25.1 2.7 %collective-permute-start = (bf16[8,256,256]{2,1,0:T(8,128)(2,1)S(1)}, bf16[8,256,256]{2,1,0:T(8,128)(2,1)S(1)}, u32[]{:S(2)}, u32[]{:S(2)}) collective-permute-start(bf16[8,256,256]{2,1,0:T(8,128)(2,1)S(1)} %all_to_all.10.own_ref), channel_id=1, source_target_pairs={{0,1},{1,0},{2,3},{3,2},{4,5},{5,4},{6,7},{7,6},{8,9},{9,8},{10,11... | collective-permute-start | bytes 3145736 | tf_op jit(solution)/shard_map/ppermute | solution.py:72
  27.7 1.0 %copy-start.2 = (bf16[8,256,256]{2,1,0:T(8,128)(2,1)}, bf16[8,256,256]{2,1,0:T(8,128)(2,1)S(1)}, u32[]{:S(2)}) copy-start(bf16[8,256,256]{2,1,0:T(8,128)(2,1)S(1)} %collective-permute-done.swapped_ref) | copy-start | bytes 3145732
  40.7 4.4 %collective-permute-start.1 = (f32[64,32,256]{2,1,0:T(8,128)}, f32[64,32,256]{2,1,0:T(8,128)S(1)}, u32[]{:S(2)}, u32[]{:S(2)}) collective-permute-start(f32[64,32,256]{2,1,0:T(8,128)} %bitcast.8), channel_id=1, source_target_pairs={{0,1},{1,0},{2,3},{3,2},{4,5},{5,4},{6,7},{7,6},{8,9},{9,8},{10,11... | collective-permute-start | bytes 6291464 | tf_op jit(solution)/shard_map/ppermute | solution.py:89

commit v10 on v9

--- a/solution.py
+++ b/solution.py
@@ -10,23 +10,21 @@
 TERM_BLOCK = 32
 
 
-def sigma_kernel(core_ref, src_ref, tgt_ref, own_ref, swapped_ref, left_ref, right_ref,
-                 mine_ref, other_ref, psi_ref):
+def sigma_kernel(core_ref, slab_ref, sector_ref, tgt_ref, own_ref, swapped_ref, left_ref,
+                 right_ref, mine_ref, other_ref):
     step = pl.program_id(0)
 
     @pl.when(step == 0)
     def _():
-        core = core_ref[0]
-        for b in range(own_ref.shape[0]):
-            psi_ref[2 * b + core] = own_ref[b]
-            psi_ref[2 * b + 1 - core] = swapped_ref[b]
         mine_ref[...] = jnp.zeros_like(mine_ref)
         other_ref[...] = jnp.zeros_like(other_ref)
 
     for j in range(TERM_BLOCK):
         t = step * TERM_BLOCK + j
+        slab = slab_ref[t]
+        psi = jnp.where(sector_ref[t] == core_ref[0], own_ref[slab], swapped_ref[slab])
         left_part = jnp.dot(
-            left_ref[j], psi_ref[src_ref[t]], preferred_element_type=jnp.float32
+            left_ref[j], psi, preferred_element_type=jnp.float32
         ).astype(jnp.bfloat16)
         term_image = lax.dot_general(
             left_part, right_ref[j], (((1,), (1,)), ((), ())),
@@ -42,7 +40,7 @@
             other_ref[target, q] += jnp.where(first, high, low)
 
 
-def add_terms(own, swapped, left_terms, right_terms, sources, targets, core, n_core, band):
+def add_terms(own, swapped, left_terms, right_terms, slab, sector, targets, core, n_core, band):
     n_slab, width, _ = own.shape
     sectors = 2 * n_slab
     n_terms = left_terms.shape[0]
@@ -54,14 +52,13 @@
         sigma_kernel,
         out_shape=(jax.ShapeDtypeStruct(out_shape, jnp.float32),) * 2,
         grid_spec=pltpu.PrefetchScalarGridSpec(
-            num_scalar_prefetch=3,
+            num_scalar_prefetch=4,
             grid=(n_terms // TERM_BLOCK,),
             in_specs=[half, half, per_step, per_step],
             out_specs=(whole, whole),
-            scratch_shapes=[pltpu.VMEM((sectors, width, width), own.dtype)],
         ),
         compiler_params=pltpu.CompilerParams(dimension_semantics=("arbitrary",)),
-    )(core, sources, targets, own, swapped, left_terms, right_terms)
+    )(core, slab, sector, targets, own, swapped, left_terms, right_terms)
 
 
 def gather_blocks(wavefunction, n_blk):
@@ -80,10 +77,12 @@
     n_rest = lax.axis_size(("y", "xh", "z", "xl"))
     width = wavefunction.shape[1]
     band = per_slab * n_blk * width // (n_core * n_rest)
-    sources = term_slab[:, 0] * per_slab + term_sector
     core = lax.axis_index("c").astype(jnp.int32).reshape(1)
     own, swapped = gather_blocks(wavefunction, n_blk)
-    mine, other = add_terms(own, swapped, left_terms, right_terms, sources, term_target, core, n_core, band)
+    mine, other = add_terms(
+        own, swapped, left_terms, right_terms, term_slab[:, 0], term_sector, term_target,
+        core, n_core, band,
+    )
     mine = mine.reshape(n_rest, band, width)
     other = other.reshape(n_rest, band, width)
     summed = mine + lax.ppermute(other, "c", [(0, 1), (1, 0)])

time: 85.2 us -> 85.1 us (level)
    unnamed x10 -> x6, local copies, waits for them, and re-layouts: 1.96 us -> 1.95 us
  transfers between devices with their start and end apart: 2 -> 2, of which waited for: 2 -> 2; matrix products, arithmetic and copies ran while one was open for 1% -> 0% of each run, Pallas kernels for 0% -> 0%
where the time goes in v10:
time: 85.1 us; the launch traced here: 84.9 us
  blocking collectives  61.2 us (72%)
  Pallas kernels  11.8 us (14%)
  waiting for transfers between devices  6.89 us (8%)
  other arithmetic  2.78 us (3%)
  local copies, waits for them, and re-layouts  2.03 us (2%)
    all_to_all x1, blocking collectives, on_device(): got = lax.all_to_all(summed, ('y', 'xh', 'z', 'xl'), 0, 0, tiled=True)  37.1 us
    all_to_all x1, blocking collectives, gather_blocks(): own = lax.all_to_all(copies, ('y', 'xh'), 0, 0, tiled=True)  24 us
    pallas_call x1, Pallas kernels, add_terms(): pl.pallas_call(sigma_kernel, out_shape=(jax.ShapeDtypeStruct(out_shape, j...  11.8 us
    ppermute x1, waiting for transfers between devices, on_device(): summed = mine + lax.ppermute(other, 'c', [(0, 1), (1, 0)])  4.23 us
    ppermute x1, waiting for transfers between devices, gather_blocks(): swapped = lax.ppermute(own, 'c', [(0, 1), (1, 0)])  2.66 us
    add x1, other arithmetic, on_device(): summed = mine + lax.ppermute(other, 'c', [(0, 1), (1, 0)])  2.03 us
    unnamed x6, local copies, waits for them, and re-layouts  1.95 us
  transfers between devices with their start and end apart: 2, of which 2 were waited for; matrix products, arithmetic and copies ran while one was open for 0% of the time, Pallas kernels for 0%

profile of v10, /device:TPU:0, one launch (start us, length us, event | category | flops | bytes accessed | tf_op | source)
XLA Modules:
  0.0 84.9 jit_solution(13452964798642231678)
XLA Ops:
  0.0 0.0 copy-start
  0.0 0.9 %copy-done = bf16[2,256,256]{2,1,0:T(8,128)(2,1)S(1)} copy-done((bf16[2,256,256]{2,1,0:T(8,128)(2,1)S(1)}, bf16[2,256,256]{2,1,0:T(8,128)(2,1)}, u32[]{:S(2)}) %copy-start) | copy-done | bytes 262168
  1.0 0.1 broadcast_in_dim.9
  1.0 24.0 %all_to_all.10.own_ref = bf16[8,256,256]{2,1,0:T(8,128)(2,1)S(1)} all-to-all(bf16[8,256,256]{2,1,0:T(8,128)(2,1)S(1)} %broadcast_in_dim.9), channel_id=1, replica_groups=mesh['y'=4,'xh'=2,'z'=4,'xl'=2,'c'=2] {'y','xh'}, dimensions={0} | all-to-all | bytes 2097152 | tf_op jit(solution)/shard_map/all_to_all | solution.py:68
  25.1 0.0 copy-start.1
  25.1 0.0 collective-permute-start
  25.1 2.7 %collective-permute-done.swapped_ref = bf16[8,256,256]{2,1,0:T(8,128)(2,1)S(1)} collective-permute-done((bf16[8,256,256]{2,1,0:T(8,128)(2,1)S(1)}, bf16[8,256,256]{2,1,0:T(8,128)(2,1)S(1)}, u32[]{:S(2)}, u32[]{:S(2)}) %collective-permute-start) | collective-permute-done | bytes 1048608 | tf_op jit(solution)/shard_map/ppermute | solution.py:69
  27.7 0.0 copy-start.2
  27.7 0.0 copy-done.1
  27.8 1.0 %copy-done.2 = bf16[8,256,256]{2,1,0:T(8,128)(2,1)} copy-done((bf16[8,256,256]{2,1,0:T(8,128)(2,1)}, bf16[8,256,256]{2,1,0:T(8,128)(2,1)S(1)}, u32[]{:S(2)}) %copy-start.2) | copy-done | bytes 1048600
  28.7 11.8 %shard_map.64 = (f32[16,4,32,256]{3,2,1,0:T(8,128)}, f32[16,4,32,256]{3,2,1,0:T(8,128)}) custom-call(s32[1]{0:T(128)} %bitcast.core_ref, s32[64]{0:T(128)} %bitcast.7, s32[64]{0:T(128)} %sector_ref.1, s32[64]{0:T(128)} %tgt_ref.1, bf16[8,256,256]{2,1,0:T(8,128)(2,1)} %copy-done.1, bf16[8,256,256]{2,1,0:T(8,128)(2,1)} %copy-done.2, ...), custom_call_target="tpu_custom_call" | custom-call | tf_op jit(solution)/shard_map/pallas_call | solution.py:51
  40.6 0.1 collective-permute-start.1
  40.7 4.2 %collective-permute-done.1 = f32[64,32,256]{2,1,0:T(8,128)S(1)} collective-permute-done((f32[64,32,256]{2,1,0:T(8,128)}, f32[64,32,256]{2,1,0:T(8,128)S(1)}, u32[]{:S(2)}, u32[]{:S(2)}) %collective-permute-start.1) | collective-permute-done | bytes 2097184 | tf_op jit(solution)/shard_map/ppermute | solution.py:88
  45.0 2.0 %bitcast_add_fusion = f32[64,32,256]{2,1,0:T(8,128)S(1)} fusion(f32[64,32,256]{2,1,0:T(8,128)S(1)} %collective-permute-done.1, f32[16,4,32,256]{3,2,1,0:T(8,128)} %get-tuple-element.7), kind=kLoop, calls=%fused_computation | loop fusion | flops 524288 | bytes 6291456 | tf_op jit(solution)/shard_map/add | solution.py:88
  47.0 37.1 %all_to_all.11 = f32[64,32,256]{2,1,0:T(8,128)S(1)} all-to-all(f32[64,32,256]{2,1,0:T(8,128)S(1)} %bitcast_add_fusion), channel_id=1, replica_groups=mesh['y'=4,'xh'=2,'z'=4,'xl'=2,'c'=2] {'y','xh','z','xl'}, dimensions={0} | all-to-all | bytes 4194304 | tf_op jit(solution)/shard_map/all_to_all | solution.py:89
  84.1 0.8 reduce_sum.9
  (1 shorter events, 0.0 us)
Async XLA Ops:
  0.0 1.0 %copy-start = (bf16[2,256,256]{2,1,0:T(8,128)(2,1)S(1)}, bf16[2,256,256]{2,1,0:T(8,128)(2,1)}, u32[]{:S(2)}) copy-start(bf16[2,256,256]{2,1,0:T(8,128)(2,1)} %param.6) | copy-start | bytes 786436
  25.1 2.7 %copy-start.1 = (bf16[8,256,256]{2,1,0:T(8,128)(2,1)}, bf16[8,256,256]{2,1,0:T(8,128)(2,1)S(1)}, u32[]{:S(2)}) copy-start(bf16[8,256,256]{2,1,0:T(8,128)(2,1)S(1)} %all_to_all.10.own_ref) | copy-start | bytes 3145732
  25.1 2.7 %collective-permute-start = (bf16[8,256,256]{2,1,0:T(8,128)(2,1)S(1)}, bf16[8,256,256]{2,1,0:T(8,128)(2,1)S(1)}, u32[]{:S(2)}, u32[]{:S(2)}) collective-permute-start(bf16[8,256,256]{2,1,0:T(8,128)(2,1)S(1)} %all_to_all.10.own_ref), channel_id=1, source_target_pairs={{0,1},{1,0},{2,3},{3,2},{4,5},{5,4},{6,7},{7,6},{8,9},{9,8},{10,11... | collective-permute-start | bytes 3145736 | tf_op jit(solution)/shard_map/ppermute | solution.py:69
  27.7 1.0 %copy-start.2 = (bf16[8,256,256]{2,1,0:T(8,128)(2,1)}, bf16[8,256,256]{2,1,0:T(8,128)(2,1)S(1)}, u32[]{:S(2)}) copy-start(bf16[8,256,256]{2,1,0:T(8,128)(2,1)S(1)} %collective-permute-done.swapped_ref) | copy-start | bytes 3145732
  40.6 4.4 %collective-permute-start.1 = (f32[64,32,256]{2,1,0:T(8,128)}, f32[64,32,256]{2,1,0:T(8,128)S(1)}, u32[]{:S(2)}, u32[]{:S(2)}) collective-permute-start(f32[64,32,256]{2,1,0:T(8,128)} %bitcast.8), channel_id=1, source_target_pairs={{0,1},{1,0},{2,3},{3,2},{4,5},{5,4},{6,7},{7,6},{8,9},{9,8},{10,11... | collective-permute-start | bytes 6291464 | tf_op jit(solution)/shard_map/ppermute | solution.py:88

commit v11 on v9

--- a/solution.py
+++ b/solution.py
@@ -7,7 +7,7 @@
 from jax.sharding import PartitionSpec as P
 
 PHYS = ("y", "xh", "z", "xl", "c")
-TERM_BLOCK = 32
+TERM_BLOCK = 16
 
 
 def sigma_kernel(core_ref, src_ref, tgt_ref, own_ref, swapped_ref, left_ref, right_ref,

time: 85.2 us -> 85.6 us (level)
  no operation moved by 1% of the time
where the time goes in v11:
time: 85.6 us; the launch traced here: 85.4 us
  blocking collectives  61.2 us (71%)
  Pallas kernels  12.4 us (14%)
  waiting for transfers between devices  6.24 us (7%)
  other arithmetic  3.41 us (4%)
  local copies, waits for them, and re-layouts  2.04 us (2%)
    all_to_all x1, blocking collectives, on_device(): got = lax.all_to_all(summed, ('y', 'xh', 'z', 'xl'), 0, 0, tiled=True)  37.1 us
    all_to_all x1, blocking collectives, gather_blocks(): own = lax.all_to_all(copies, ('y', 'xh'), 0, 0, tiled=True)  24 us
    pallas_call x1, Pallas kernels, add_terms(): pl.pallas_call(sigma_kernel, out_shape=(jax.ShapeDtypeStruct(out_shape, j...  12.4 us
    ppermute x1, waiting for transfers between devices, on_device(): summed = mine + lax.ppermute(other, 'c', [(0, 1), (1, 0)])  4.23 us
    add x1, other arithmetic, on_device(): summed = mine + lax.ppermute(other, 'c', [(0, 1), (1, 0)])  2.03 us
    ppermute x1, waiting for transfers between devices, gather_blocks(): swapped = lax.ppermute(own, 'c', [(0, 1), (1, 0)])  2.01 us
    unnamed x10, local copies, waits for them, and re-layouts  1.96 us
  transfers between devices with their start and end apart: 2, of which 2 were waited for; matrix products, arithmetic and copies ran while one was open for 1% of the time, Pallas kernels for 0%

profile of v11, /device:TPU:0, one launch (start us, length us, event | category | flops | bytes accessed | tf_op | source)
XLA Modules:
  0.0 85.4 jit_solution(15622298172308878372)
XLA Ops:
  0.0 0.0 copy-start
  0.0 0.0 copy-start.3
  0.0 0.0 copy-start.4
  0.0 0.9 %copy-done = bf16[2,256,256]{2,1,0:T(8,128)(2,1)S(1)} copy-done((bf16[2,256,256]{2,1,0:T(8,128)(2,1)S(1)}, bf16[2,256,256]{2,1,0:T(8,128)(2,1)}, u32[]{:S(2)}) %copy-start) | copy-done | bytes 262168
  1.0 0.1 broadcast_in_dim.9
  1.0 24.0 %all_to_all.10.own_ref = bf16[8,256,256]{2,1,0:T(8,128)(2,1)S(1)} all-to-all(bf16[8,256,256]{2,1,0:T(8,128)(2,1)S(1)} %broadcast_in_dim.9), channel_id=1, replica_groups=mesh['y'=4,'xh'=2,'z'=4,'xl'=2,'c'=2] {'y','xh'}, dimensions={0} | all-to-all | bytes 2097152 | tf_op jit(solution)/shard_map/all_to_all | solution.py:71
  25.1 0.0 copy-start.1
  25.1 0.0 collective-permute-start
  25.1 0.0 copy-done.3
  25.1 0.0 copy-done.4
  25.1 0.6 bitcast_add_fusion.1.src_ref
  25.7 2.0 %collective-permute-done.swapped_ref = bf16[8,256,256]{2,1,0:T(8,128)(2,1)S(1)} collective-permute-done((bf16[8,256,256]{2,1,0:T(8,128)(2,1)S(1)}, bf16[8,256,256]{2,1,0:T(8,128)(2,1)S(1)}, u32[]{:S(2)}, u32[]{:S(2)}) %collective-permute-start) | collective-permute-done | bytes 1048608 | tf_op jit(solution)/shard_map/ppermute | solution.py:72
  27.7 0.0 copy-start.2
  27.7 0.0 copy-done.1
  27.8 1.0 %copy-done.2 = bf16[8,256,256]{2,1,0:T(8,128)(2,1)} copy-done((bf16[8,256,256]{2,1,0:T(8,128)(2,1)}, bf16[8,256,256]{2,1,0:T(8,128)(2,1)S(1)}, u32[]{:S(2)}) %copy-start.2) | copy-done | bytes 1048600
  28.8 12.4 %shard_map.64 = (f32[16,4,32,256]{3,2,1,0:T(8,128)}, f32[16,4,32,256]{3,2,1,0:T(8,128)}) custom-call(s32[1]{0:T(128)} %bitcast.core_ref, s32[64]{0:T(128)} %bitcast_add_fusion.1.src_ref, s32[64]{0:T(128)} %tgt_ref.1, bf16[8,256,256]{2,1,0:T(8,128)(2,1)} %copy-done.1, bf16[8,256,256]{2,1,0:T(8,128)(2,1)} %copy-done.2, bf16[64,256,256]{2,1,0:T(8,128)(2,1)} %left_ref.1, ...), custom_call_target="tpu_custom_call" | custom-call | tf_op jit(solution)/shard_map/pallas_call | solution.py:53
  41.1 0.1 collective-permute-start.1
  41.3 4.2 %collective-permute-done.1 = f32[64,32,256]{2,1,0:T(8,128)S(1)} collective-permute-done((f32[64,32,256]{2,1,0:T(8,128)}, f32[64,32,256]{2,1,0:T(8,128)S(1)}, u32[]{:S(2)}, u32[]{:S(2)}) %collective-permute-start.1) | collective-permute-done | bytes 2097184 | tf_op jit(solution)/shard_map/ppermute | solution.py:89
  45.5 2.0 %bitcast_add_fusion = f32[64,32,256]{2,1,0:T(8,128)S(1)} fusion(f32[64,32,256]{2,1,0:T(8,128)S(1)} %collective-permute-done.1, f32[16,4,32,256]{3,2,1,0:T(8,128)} %get-tuple-element.7), kind=kLoop, calls=%fused_computation | loop fusion | flops 524288 | bytes 6291456 | tf_op jit(solution)/shard_map/add | solution.py:89
  47.5 37.1 %all_to_all.11 = f32[64,32,256]{2,1,0:T(8,128)S(1)} all-to-all(f32[64,32,256]{2,1,0:T(8,128)S(1)} %bitcast_add_fusion), channel_id=1, replica_groups=mesh['y'=4,'xh'=2,'z'=4,'xl'=2,'c'=2] {'y','xh','z','xl'}, dimensions={0} | all-to-all | bytes 4194304 | tf_op jit(solution)/shard_map/all_to_all | solution.py:90
  84.6 0.8 reduce_sum.9
  (1 shorter events, 0.0 us)
Async XLA Ops:
  0.0 1.0 %copy-start = (bf16[2,256,256]{2,1,0:T(8,128)(2,1)S(1)}, bf16[2,256,256]{2,1,0:T(8,128)(2,1)}, u32[]{:S(2)}) copy-start(bf16[2,256,256]{2,1,0:T(8,128)(2,1)} %param.6) | copy-start | bytes 786436
  0.0 25.1 %copy-start.3 = (s32[64]{0:T(128)S(1)}, s32[64]{0:T(128)}, u32[]{:S(2)}) copy-start(s32[64]{0:T(128)} %param.10) | copy-start | bytes 772
  0.0 25.1 %copy-start.4 = (s32[64,1]{0,1:T(1,128)S(1)}, s32[64,1]{0,1:T(1,128)}, u32[]{:S(2)}) copy-start(s32[64,1]{0,1:T(1,128)} %param.9) | copy-start | bytes 772
  25.1 2.7 %copy-start.1 = (bf16[8,256,256]{2,1,0:T(8,128)(2,1)}, bf16[8,256,256]{2,1,0:T(8,128)(2,1)S(1)}, u32[]{:S(2)}) copy-start(bf16[8,256,256]{2,1,0:T(8,128)(2,1)S(1)} %all_to_all.10.own_ref) | copy-start | bytes 3145732
  25.1 2.7 %collective-permute-start = (bf16[8,256,256]{2,1,0:T(8,128)(2,1)S(1)}, bf16[8,256,256]{2,1,0:T(8,128)(2,1)S(1)}, u32[]{:S(2)}, u32[]{:S(2)}) collective-permute-start(bf16[8,256,256]{2,1,0:T(8,128)(2,1)S(1)} %all_to_all.10.own_ref), channel_id=1, source_target_pairs={{0,1},{1,0},{2,3},{3,2},{4,5},{5,4},{6,7},{7,6},{8,9},{9,8},{10,11... | collective-permute-start | bytes 3145736 | tf_op jit(solution)/shard_map/ppermute | solution.py:72
  27.7 1.0 %copy-start.2 = (bf16[8,256,256]{2,1,0:T(8,128)(2,1)}, bf16[8,256,256]{2,1,0:T(8,128)(2,1)S(1)}, u32[]{:S(2)}) copy-start(bf16[8,256,256]{2,1,0:T(8,128)(2,1)S(1)} %collective-permute-done.swapped_ref) | copy-start | bytes 3145732
  41.1 4.4 %collective-permute-start.1 = (f32[64,32,256]{2,1,0:T(8,128)}, f32[64,32,256]{2,1,0:T(8,128)S(1)}, u32[]{:S(2)}, u32[]{:S(2)}) collective-permute-start(f32[64,32,256]{2,1,0:T(8,128)} %bitcast.8), channel_id=1, source_target_pairs={{0,1},{1,0},{2,3},{3,2},{4,5},{5,4},{6,7},{7,6},{8,9},{9,8},{10,11... | collective-permute-start | bytes 6291464 | tf_op jit(solution)/shard_map/ppermute | solution.py:89

commit v12 on v9

--- a/solution.py
+++ b/solution.py
@@ -86,7 +86,11 @@
     mine, other = add_terms(own, swapped, left_terms, right_terms, sources, term_target, core, n_core, band)
     mine = mine.reshape(n_rest, band, width)
     other = other.reshape(n_rest, band, width)
-    summed = mine + lax.ppermute(other, "c", [(0, 1), (1, 0)])
+    half = n_rest // 2
+    swap = [(0, 1), (1, 0)]
+    first = lax.ppermute(other[:half], "c", swap)
+    second = lax.ppermute(other[half:], "c", swap)
+    summed = mine + jnp.concatenate([first, second], 0)
     got = lax.all_to_all(summed, ("y", "xh", "z", "xl"), 0, 0, tiled=True)
     return got.sum(0)
 

time: 85.2 us -> 85.5 us (level)
  local copies, waits for them, and re-layouts: 2.04 us -> 3.87 us
  other arithmetic: 3.41 us -> 1.91 us
    slice x0 -> x1, local copies, waits for them, and re-layouts: none -> 1.83 us  [on_device(): first = lax.ppermute(other[:half], 'c', swap)]
    add x1, other arithmetic: 2.03 us -> 0.6 us  [on_device(): summed = mine + jnp.concatenate([first, second], 0)]
    ppermute x1 -> x2, waiting for transfers between devices: 4.24 us -> 3.65 us  [the longest x1 2.15 us: on_device(): second = lax.ppermute(other[half:], 'c', swap)]
    unnamed x10 -> x12, local copies, waits for them, and re-layouts: 1.96 us -> 1.97 us
  transfers between devices with their start and end apart: 2 -> 3, of which waited for: 2 -> 3; matrix products, arithmetic and copies ran while one was open for 1% -> 1% of each run, Pallas kernels for 0% -> 0%
where the time goes in v12:
time: 85.5 us; the launch traced here: 85.3 us
  blocking collectives  61.2 us (72%)
  Pallas kernels  12 us (14%)
  waiting for transfers between devices  5.73 us (7%)
  local copies, waits for them, and re-layouts  3.87 us (5%)
  other arithmetic  1.91 us (2%)
    all_to_all x1, blocking collectives, on_device(): got = lax.all_to_all(summed, ('y', 'xh', 'z', 'xl'), 0, 0, tiled=True)  37.1 us
    all_to_all x1, blocking collectives, gather_blocks(): own = lax.all_to_all(copies, ('y', 'xh'), 0, 0, tiled=True)  24 us
    pallas_call x1, Pallas kernels, add_terms(): pl.pallas_call(sigma_kernel, out_shape=(jax.ShapeDtypeStruct(out_shape, j...  12 us
    ppermute x1, waiting for transfers between devices, on_device(): second = lax.ppermute(other[half:], 'c', swap)  2.15 us
    ppermute x1, waiting for transfers between devices, gather_blocks(): swapped = lax.ppermute(own, 'c', [(0, 1), (1, 0)])  2.08 us
    unnamed x12, local copies, waits for them, and re-layouts  1.97 us
    slice x1, local copies, waits for them, and re-layouts, on_device(): first = lax.ppermute(other[:half], 'c', swap)  1.83 us
  transfers between devices with their start and end apart: 3, of which 3 were waited for; matrix products, arithmetic and copies ran while one was open for 1% of the time, Pallas kernels for 0%

profile of v12, /device:TPU:0, one launch (start us, length us, event | category | flops | bytes accessed | tf_op | source)
XLA Modules:
  0.0 85.3 jit_solution(4528758726510647595)
XLA Ops:
  0.0 0.0 copy-start
  0.0 0.0 copy-start.4
  0.0 0.0 copy-start.5
  0.0 0.9 %copy-done = bf16[2,256,256]{2,1,0:T(8,128)(2,1)S(1)} copy-done((bf16[2,256,256]{2,1,0:T(8,128)(2,1)S(1)}, bf16[2,256,256]{2,1,0:T(8,128)(2,1)}, u32[]{:S(2)}) %copy-start) | copy-done | bytes 262168
  1.0 0.1 broadcast_in_dim.9
  1.0 24.0 %all_to_all.10.own_ref = bf16[8,256,256]{2,1,0:T(8,128)(2,1)S(1)} all-to-all(bf16[8,256,256]{2,1,0:T(8,128)(2,1)S(1)} %broadcast_in_dim.9), channel_id=1, replica_groups=mesh['y'=4,'xh'=2,'z'=4,'xl'=2,'c'=2] {'y','xh'}, dimensions={0} | all-to-all | bytes 2097152 | tf_op jit(solution)/shard_map/all_to_all | solution.py:71
  25.1 0.0 copy-start.1
  25.1 0.0 collective-permute-start
  25.1 0.0 copy-done.4
  25.1 0.0 copy-done.5
  25.1 0.6 bitcast_add_fusion.src_ref
  25.7 2.1 %collective-permute-done.swapped_ref = bf16[8,256,256]{2,1,0:T(8,128)(2,1)S(1)} collective-permute-done((bf16[8,256,256]{2,1,0:T(8,128)(2,1)S(1)}, bf16[8,256,256]{2,1,0:T(8,128)(2,1)S(1)}, u32[]{:S(2)}, u32[]{:S(2)}) %collective-permute-start) | collective-permute-done | bytes 1048608 | tf_op jit(solution)/shard_map/ppermute | solution.py:72
  27.7 0.0 copy-start.3
  27.7 0.0 copy-done.1
  27.8 1.0 %copy-done.3 = bf16[8,256,256]{2,1,0:T(8,128)(2,1)} copy-done((bf16[8,256,256]{2,1,0:T(8,128)(2,1)}, bf16[8,256,256]{2,1,0:T(8,128)(2,1)S(1)}, u32[]{:S(2)}) %copy-start.3) | copy-done | bytes 1048600
  28.8 12.0 %shard_map.64 = (f32[16,4,32,256]{3,2,1,0:T(8,128)}, f32[16,4,32,256]{3,2,1,0:T(8,128)}) custom-call(s32[1]{0:T(128)} %bitcast.core_ref, s32[64]{0:T(128)} %bitcast_add_fusion.src_ref, s32[64]{0:T(128)} %tgt_ref.1, bf16[8,256,256]{2,1,0:T(8,128)(2,1)} %copy-done.1, bf16[8,256,256]{2,1,0:T(8,128)(2,1)} %copy-done.3, bf16[64,256,256]{2,1,0:T(8,128)(2,1)} %left_ref.1, ...), custom_call_target="tpu_custom_call" | custom-call | tf_op jit(solution)/shard_map/pallas_call | solution.py:53
  40.7 0.0 copy-start.2
  40.7 1.8 %fusion = (f32[8,4,32,256]{3,2,1,0:T(8,128)S(1)}, f32[8,4,32,256]{3,2,1,0:T(8,128)S(1)}) fusion(f32[16,4,32,256]{3,2,1,0:T(8,128)} %get-tuple-element.8), kind=kLoop, calls=%fused_computation.3 | loop fusion | bytes 4194304 | tf_op jit(solution)/shard_map/slice | solution.py:91
  42.5 0.2 collective-permute-start.2
  42.8 0.4 collective-permute-start.1
  43.1 2.1 %collective-permute-done.2 = f32[32,32,256]{2,1,0:T(8,128)S(1)} collective-permute-done((f32[32,32,256]{2,1,0:T(8,128)S(1)}, f32[32,32,256]{2,1,0:T(8,128)S(1)}, u32[]{:S(2)}, u32[]{:S(2)}) %collective-permute-start.2) | collective-permute-done | bytes 1048608 | tf_op jit(solution)/shard_map/ppermute | solution.py:92
  45.3 1.5 %collective-permute-done.1 = f32[32,32,256]{2,1,0:T(8,128)S(1)} collective-permute-done((f32[32,32,256]{2,1,0:T(8,128)S(1)}, f32[32,32,256]{2,1,0:T(8,128)S(1)}, u32[]{:S(2)}, u32[]{:S(2)}) %collective-permute-start.1) | collective-permute-done | bytes 1048608 | tf_op jit(solution)/shard_map/ppermute | solution.py:91
  46.8 0.0 copy-done.2
  46.8 0.6 maximum_add_fusion
  47.4 37.1 %all_to_all.11 = f32[64,32,256]{2,1,0:T(8,128)S(1)} all-to-all(f32[64,32,256]{2,1,0:T(8,128)S(1)} %maximum_add_fusion), channel_id=1, replica_groups=mesh['y'=4,'xh'=2,'z'=4,'xl'=2,'c'=2] {'y','xh','z','xl'}, dimensions={0} | all-to-all | bytes 4194304 | tf_op jit(solution)/shard_map/all_to_all | solution.py:94
  84.5 0.8 reduce_sum.9
  (1 shorter events, 0.0 us)
Async XLA Ops:
  0.0 1.0 %copy-start = (bf16[2,256,256]{2,1,0:T(8,128)(2,1)S(1)}, bf16[2,256,256]{2,1,0:T(8,128)(2,1)}, u32[]{:S(2)}) copy-start(bf16[2,256,256]{2,1,0:T(8,128)(2,1)} %param.6) | copy-start | bytes 786436
  0.0 25.1 %copy-start.4 = (s32[64]{0:T(128)S(1)}, s32[64]{0:T(128)}, u32[]{:S(2)}) copy-start(s32[64]{0:T(128)} %param.10) | copy-start | bytes 772
  0.0 25.1 %copy-start.5 = (s32[64,1]{0,1:T(1,128)S(1)}, s32[64,1]{0,1:T(1,128)}, u32[]{:S(2)}) copy-start(s32[64,1]{0,1:T(1,128)} %param.9) | copy-start | bytes 772
  25.1 2.7 %copy-start.1 = (bf16[8,256,256]{2,1,0:T(8,128)(2,1)}, bf16[8,256,256]{2,1,0:T(8,128)(2,1)S(1)}, u32[]{:S(2)}) copy-start(bf16[8,256,256]{2,1,0:T(8,128)(2,1)S(1)} %all_to_all.10.own_ref) | copy-start | bytes 3145732
  25.1 2.7 %collective-permute-start = (bf16[8,256,256]{2,1,0:T(8,128)(2,1)S(1)}, bf16[8,256,256]{2,1,0:T(8,128)(2,1)S(1)}, u32[]{:S(2)}, u32[]{:S(2)}) collective-permute-start(bf16[8,256,256]{2,1,0:T(8,128)(2,1)S(1)} %all_to_all.10.own_ref), channel_id=1, source_target_pairs={{0,1},{1,0},{2,3},{3,2},{4,5},{5,4},{6,7},{7,6},{8,9},{9,8},{10,11... | collective-permute-start | bytes 3145736 | tf_op jit(solution)/shard_map/ppermute | solution.py:72
  27.7 1.0 %copy-start.3 = (bf16[8,256,256]{2,1,0:T(8,128)(2,1)}, bf16[8,256,256]{2,1,0:T(8,128)(2,1)S(1)}, u32[]{:S(2)}) copy-start(bf16[8,256,256]{2,1,0:T(8,128)(2,1)S(1)} %collective-permute-done.swapped_ref) | copy-start | bytes 3145732
  40.7 6.1 %copy-start.2 = (f32[16,4,32,256]{3,2,1,0:T(8,128)S(1)}, f32[16,4,32,256]{3,2,1,0:T(8,128)}, u32[]{:S(2)}) copy-start(f32[16,4,32,256]{3,2,1,0:T(8,128)} %get-tuple-element.7) | copy-start | bytes 6291460
  42.5 2.7 %collective-permute-start.2 = (f32[32,32,256]{2,1,0:T(8,128)S(1)}, f32[32,32,256]{2,1,0:T(8,128)S(1)}, u32[]{:S(2)}, u32[]{:S(2)}) collective-permute-start(f32[32,32,256]{2,1,0:T(8,128)S(1)} %bitcast.10), channel_id=1, source_target_pairs={{0,1},{1,0},{2,3},{3,2},{4,5},{5,4},{6,7},{7,6},{8,9},{9,8},{10,11... | collective-permute-start | bytes 3145736 | tf_op jit(solution)/shard_map/ppermute | solution.py:92
  42.8 4.0 %collective-permute-start.1 = (f32[32,32,256]{2,1,0:T(8,128)S(1)}, f32[32,32,256]{2,1,0:T(8,128)S(1)}, u32[]{:S(2)}, u32[]{:S(2)}) collective-permute-start(f32[32,32,256]{2,1,0:T(8,128)S(1)} %bitcast.9), channel_id=1, source_target_pairs={{0,1},{1,0},{2,3},{3,2},{4,5},{5,4},{6,7},{7,6},{8,9},{9,8},{10,11... | collective-permute-start | bytes 3145736 | tf_op jit(solution)/shard_map/ppermute | solution.py:91

commit v13 on v9

--- a/solution.py
+++ b/solution.py
@@ -11,7 +11,7 @@
 
 
 def sigma_kernel(core_ref, src_ref, tgt_ref, own_ref, swapped_ref, left_ref, right_ref,
-                 mine_ref, other_ref, psi_ref):
+                 mine_ref, other_lo_ref, other_hi_ref, psi_ref):
     step = pl.program_id(0)
 
     @pl.when(step == 0)
@@ -21,7 +21,8 @@
             psi_ref[2 * b + core] = own_ref[b]
             psi_ref[2 * b + 1 - core] = swapped_ref[b]
         mine_ref[...] = jnp.zeros_like(mine_ref)
-        other_ref[...] = jnp.zeros_like(other_ref)
+        other_lo_ref[...] = jnp.zeros_like(other_lo_ref)
+        other_hi_ref[...] = jnp.zeros_like(other_hi_ref)
 
     for j in range(TERM_BLOCK):
         t = step * TERM_BLOCK + j
@@ -33,31 +34,42 @@
             preferred_element_type=jnp.float32,
         )
         _, bands, band, _ = mine_ref.shape
+        split = other_lo_ref.shape[1]
         target = tgt_ref[t]
         first = core_ref[0] == 0
         for q in range(bands):
             low = term_image[2 * q * band:(2 * q + 1) * band]
             high = term_image[(2 * q + 1) * band:(2 * q + 2) * band]
             mine_ref[target, q] += jnp.where(first, low, high)
-            other_ref[target, q] += jnp.where(first, high, low)
+            if q < split:
+                other_lo_ref[target, q] += jnp.where(first, high, low)
+            else:
+                other_hi_ref[target, q - split] += jnp.where(first, high, low)
 
 
 def add_terms(own, swapped, left_terms, right_terms, sources, targets, core, n_core, band):
     n_slab, width, _ = own.shape
     sectors = 2 * n_slab
     n_terms = left_terms.shape[0]
-    out_shape = (sectors, width // (n_core * band), band, width)
+    bands = width // (n_core * band)
+    out_shape = (sectors, bands, band, width)
+    half_shape = (sectors, bands // 2, band, width)
     half = pl.BlockSpec((n_slab, width, width), lambda i, *_: (0, 0, 0))
     whole = pl.BlockSpec(out_shape, lambda i, *_: (0,) * len(out_shape))
+    halves = pl.BlockSpec(half_shape, lambda i, *_: (0,) * len(half_shape))
     per_step = pl.BlockSpec((TERM_BLOCK, width, width), lambda i, *_: (i, 0, 0))
     return pl.pallas_call(
         sigma_kernel,
-        out_shape=(jax.ShapeDtypeStruct(out_shape, jnp.float32),) * 2,
+        out_shape=(
+            jax.ShapeDtypeStruct(out_shape, jnp.float32),
+            jax.ShapeDtypeStruct(half_shape, jnp.float32),
+            jax.ShapeDtypeStruct(half_shape, jnp.float32),
+        ),
         grid_spec=pltpu.PrefetchScalarGridSpec(
             num_scalar_prefetch=3,
             grid=(n_terms // TERM_BLOCK,),
             in_specs=[half, half, per_step, per_step],
-            out_specs=(whole, whole),
+            out_specs=(whole, halves, halves),
             scratch_shapes=[pltpu.VMEM((sectors, width, width), own.dtype)],
         ),
         compiler_params=pltpu.CompilerParams(dimension_semantics=("arbitrary",)),
@@ -83,10 +95,14 @@
     sources = term_slab[:, 0] * per_slab + term_sector
     core = lax.axis_index("c").astype(jnp.int32).reshape(1)
     own, swapped = gather_blocks(wavefunction, n_blk)
-    mine, other = add_terms(own, swapped, left_terms, right_terms, sources, term_target, core, n_core, band)
-    mine = mine.reshape(n_rest, band, width)
-    other = other.reshape(n_rest, band, width)
-    summed = mine + lax.ppermute(other, "c", [(0, 1), (1, 0)])
+    mine, other_lo, other_hi = add_terms(
+        own, swapped, left_terms, right_terms, sources, term_target, core, n_core, band
+    )
+    swap = [(0, 1), (1, 0)]
+    received = jnp.concatenate(
+        [lax.ppermute(other_lo, "c", swap), lax.ppermute(other_hi, "c", swap)], 1
+    )
+    summed = (mine + received).reshape(n_rest, band, width)
     got = lax.all_to_all(summed, ("y", "xh", "z", "xl"), 0, 0, tiled=True)
     return got.sum(0)
 

time: 85.2 us -> 85.1 us (level)
    ppermute x1 -> x2, waiting for transfers between devices: 4.24 us -> 3.86 us  [the longest x1 2.36 us: on_device(): lax.ppermute(other_lo, 'c', swap)]
  transfers between devices with their start and end apart: 2 -> 3, of which waited for: 2 -> 3; matrix products, arithmetic and copies ran while one was open for 1% -> 1% of each run, Pallas kernels for 0% -> 0%
where the time goes in v13:
time: 85.1 us; the launch traced here: 84.9 us
  blocking collectives  61.2 us (72%)
  Pallas kernels  11.9 us (14%)
  waiting for transfers between devices  5.93 us (7%)
  other arithmetic  3.31 us (4%)
  local copies, waits for them, and re-layouts  2.02 us (2%)
    all_to_all x1, blocking collectives, on_device(): got = lax.all_to_all(summed, ('y', 'xh', 'z', 'xl'), 0, 0, tiled=True)  37.1 us
    all_to_all x1, blocking collectives, gather_blocks(): own = lax.all_to_all(copies, ('y', 'xh'), 0, 0, tiled=True)  24 us
    pallas_call x1, Pallas kernels, add_terms(): pl.pallas_call(sigma_kernel, out_shape=(jax.ShapeDtypeStruct(out_shape, j...  11.9 us
    ppermute x1, waiting for transfers between devices, on_device(): lax.ppermute(other_lo, 'c', swap)  2.36 us
    ppermute x1, waiting for transfers between devices, gather_blocks(): swapped = lax.ppermute(own, 'c', [(0, 1), (1, 0)])  2.07 us
    add x1, other arithmetic, on_device(): summed = (mine + received).reshape(n_rest, band, width)  1.98 us
    unnamed x10, local copies, waits for them, and re-layouts  1.94 us
  transfers between devices with their start and end apart: 3, of which 3 were waited for; matrix products, arithmetic and copies ran while one was open for 1% of the time, Pallas kernels for 0%

profile of v13, /device:TPU:0, one launch (start us, length us, event | category | flops | bytes accessed | tf_op | source)
XLA Modules:
  0.0 84.9 jit_solution(2219411518224397486)
XLA Ops:
  0.0 0.0 copy-start
  0.0 0.0 copy-start.3
  0.0 0.0 copy-start.4
  0.0 0.9 %copy-done = bf16[2,256,256]{2,1,0:T(8,128)(2,1)S(1)} copy-done((bf16[2,256,256]{2,1,0:T(8,128)(2,1)S(1)}, bf16[2,256,256]{2,1,0:T(8,128)(2,1)}, u32[]{:S(2)}) %copy-start) | copy-done | bytes 262168
  1.0 0.1 broadcast_in_dim.9
  1.0 24.0 %all_to_all.10.own_ref = bf16[8,256,256]{2,1,0:T(8,128)(2,1)S(1)} all-to-all(bf16[8,256,256]{2,1,0:T(8,128)(2,1)S(1)} %broadcast_in_dim.9), channel_id=1, replica_groups=mesh['y'=4,'xh'=2,'z'=4,'xl'=2,'c'=2] {'y','xh'}, dimensions={0} | all-to-all | bytes 2097152 | tf_op jit(solution)/shard_map/all_to_all | solution.py:83
  25.1 0.0 copy-start.1
  25.1 0.0 collective-permute-start
  25.1 0.0 copy-done.3
  25.1 0.0 copy-done.4
  25.1 0.6 bitcast_add_fusion.src_ref
  25.7 2.1 %collective-permute-done.swapped_ref = bf16[8,256,256]{2,1,0:T(8,128)(2,1)S(1)} collective-permute-done((bf16[8,256,256]{2,1,0:T(8,128)(2,1)S(1)}, bf16[8,256,256]{2,1,0:T(8,128)(2,1)S(1)}, u32[]{:S(2)}, u32[]{:S(2)}) %collective-permute-start) | collective-permute-done | bytes 1048608 | tf_op jit(solution)/shard_map/ppermute | solution.py:84
  27.7 0.0 copy-start.2
  27.7 0.0 copy-done.1
  27.8 1.0 %copy-done.2 = bf16[8,256,256]{2,1,0:T(8,128)(2,1)} copy-done((bf16[8,256,256]{2,1,0:T(8,128)(2,1)}, bf16[8,256,256]{2,1,0:T(8,128)(2,1)S(1)}, u32[]{:S(2)}) %copy-start.2) | copy-done | bytes 1048600
  28.7 11.9 %shard_map.64 = (f32[16,4,32,256]{3,2,1,0:T(8,128)}, f32[16,2,32,256]{3,2,1,0:T(8,128)}, f32[16,2,32,256]{3,2,1,0:T(8,128)}) custom-call(s32[1]{0:T(128)} %bitcast.core_ref, s32[64]{0:T(128)} %bitcast_add_fusion.src_ref, s32[64]{0:T(128)} %tgt_ref.1, bf16[8,256,256]{2,1,0:T(8,128)(2,1)} %copy-done.1, bf16[8,256,256]{2,1,0:T(8,128)(2,1)} %copy-done.2, ...), custom_call_target="tpu_custom_call" | custom-call | tf_op jit(solution)/shard_map/pallas_call | solution.py:61
  40.7 0.1 collective-permute-start.1
  40.8 0.4 collective-permute-start.2
  41.2 2.4 %collective-permute-done.1 = f32[16,2,32,256]{3,2,1,0:T(8,128)S(1)} collective-permute-done((f32[16,2,32,256]{3,2,1,0:T(8,128)}, f32[16,2,32,256]{3,2,1,0:T(8,128)S(1)}, u32[]{:S(2)}, u32[]{:S(2)}) %collective-permute-start.1) | collective-permute-done | bytes 1048608 | tf_op jit(solution)/shard_map/ppermute | solution.py:103
  43.5 1.5 %collective-permute-done.2 = f32[16,2,32,256]{3,2,1,0:T(8,128)S(1)} collective-permute-done((f32[16,2,32,256]{3,2,1,0:T(8,128)}, f32[16,2,32,256]{3,2,1,0:T(8,128)S(1)}, u32[]{:S(2)}, u32[]{:S(2)}) %collective-permute-start.2) | collective-permute-done | bytes 1048608 | tf_op jit(solution)/shard_map/ppermute | solution.py:103
  45.0 2.0 %maximum_add_fusion = f32[16,4,32,256]{3,2,1,0:T(8,128)S(1)} fusion(f32[16,4,32,256]{3,2,1,0:T(8,128)} %get-tuple-element.8, f32[16,2,32,256]{3,2,1,0:T(8,128)S(1)} %collective-permute-done.2, f32[16,2,32,256]{3,2,1,0:T(8,128)S(1)} %collective-permute-done.1), kind=kLoop, calls=%fused_computation | loop fusion | flops 1048576 | bytes 6291456 | tf_op jit(solution)/shard_map/add | solution.py:105
  47.0 37.1 %all_to_all.11 = f32[64,32,256]{2,1,0:T(8,128)S(1)} all-to-all(f32[64,32,256]{2,1,0:T(8,128)S(1)} %bitcast.6), channel_id=1, replica_groups=mesh['y'=4,'xh'=2,'z'=4,'xl'=2,'c'=2] {'y','xh','z','xl'}, dimensions={0} | all-to-all | bytes 4194304 | tf_op jit(solution)/shard_map/all_to_all | solution.py:106
  84.1 0.8 reduce_sum.9
  (1 shorter events, 0.0 us)
Async XLA Ops:
  0.0 1.0 %copy-start = (bf16[2,256,256]{2,1,0:T(8,128)(2,1)S(1)}, bf16[2,256,256]{2,1,0:T(8,128)(2,1)}, u32[]{:S(2)}) copy-start(bf16[2,256,256]{2,1,0:T(8,128)(2,1)} %param.6) | copy-start | bytes 786436
  0.0 25.1 %copy-start.3 = (s32[64]{0:T(128)S(1)}, s32[64]{0:T(128)}, u32[]{:S(2)}) copy-start(s32[64]{0:T(128)} %param.10) | copy-start | bytes 772
  0.0 25.1 %copy-start.4 = (s32[64,1]{0,1:T(1,128)S(1)}, s32[64,1]{0,1:T(1,128)}, u32[]{:S(2)}) copy-start(s32[64,1]{0,1:T(1,128)} %param.9) | copy-start | bytes 772
  25.1 2.7 %copy-start.1 = (bf16[8,256,256]{2,1,0:T(8,128)(2,1)}, bf16[8,256,256]{2,1,0:T(8,128)(2,1)S(1)}, u32[]{:S(2)}) copy-start(bf16[8,256,256]{2,1,0:T(8,128)(2,1)S(1)} %all_to_all.10.own_ref) | copy-start | bytes 3145732
  25.1 2.7 %collective-permute-start = (bf16[8,256,256]{2,1,0:T(8,128)(2,1)S(1)}, bf16[8,256,256]{2,1,0:T(8,128)(2,1)S(1)}, u32[]{:S(2)}, u32[]{:S(2)}) collective-permute-start(bf16[8,256,256]{2,1,0:T(8,128)(2,1)S(1)} %all_to_all.10.own_ref), channel_id=1, source_target_pairs={{0,1},{1,0},{2,3},{3,2},{4,5},{5,4},{6,7},{7,6},{8,9},{9,8},{10,11... | collective-permute-start | bytes 3145736 | tf_op jit(solution)/shard_map/ppermute | solution.py:84
  27.7 1.0 %copy-start.2 = (bf16[8,256,256]{2,1,0:T(8,128)(2,1)}, bf16[8,256,256]{2,1,0:T(8,128)(2,1)S(1)}, u32[]{:S(2)}) copy-start(bf16[8,256,256]{2,1,0:T(8,128)(2,1)S(1)} %collective-permute-done.swapped_ref) | copy-start | bytes 3145732
  40.7 2.9 %collective-permute-start.1 = (f32[16,2,32,256]{3,2,1,0:T(8,128)}, f32[16,2,32,256]{3,2,1,0:T(8,128)S(1)}, u32[]{:S(2)}, u32[]{:S(2)}) collective-permute-start(f32[16,2,32,256]{3,2,1,0:T(8,128)} %get-tuple-element.9), channel_id=1, source_target_pairs={{0,1},{1,0},{2,3},{3,2},{4,5},{5,4},{6,7},{7,6},{8,9},{9,8},{10,11... | collective-permute-start | bytes 3145736 | tf_op jit(solution)/shard_map/ppermute | solution.py:103
  40.8 4.2 %collective-permute-start.2 = (f32[16,2,32,256]{3,2,1,0:T(8,128)}, f32[16,2,32,256]{3,2,1,0:T(8,128)S(1)}, u32[]{:S(2)}, u32[]{:S(2)}) collective-permute-start(f32[16,2,32,256]{3,2,1,0:T(8,128)} %get-tuple-element.10), channel_id=1, source_target_pairs={{0,1},{1,0},{2,3},{3,2},{4,5},{5,4},{6,7},{7,6},{8,9},{9,8},{10,11... | collective-permute-start | bytes 3145736 | tf_op jit(solution)/shard_map/ppermute | solution.py:103

commit v14 on v9

--- a/solution.py
+++ b/solution.py
@@ -85,6 +85,7 @@
     own, swapped = gather_blocks(wavefunction, n_blk)
     mine, other = add_terms(own, swapped, left_terms, right_terms, sources, term_target, core, n_core, band)
     mine = mine.reshape(n_rest, band, width)
+    mine = lax.optimization_barrier(jnp.where(mine == mine, mine, 0.0))
     other = other.reshape(n_rest, band, width)
     summed = mine + lax.ppermute(other, "c", [(0, 1), (1, 0)])
     got = lax.all_to_all(summed, ("y", "xh", "z", "xl"), 0, 0, tiled=True)

time: 85.2 us -> 83.7 us (0.982)
  waiting for transfers between devices: 6.25 us -> 4.35 us
    ppermute x1, waiting for transfers between devices: 4.24 us -> 2.34 us  [on_device(): summed = mine + lax.ppermute(other, 'c', [(0, 1), (1, 0)])]
    select_n x0 -> x1, other arithmetic: none -> 1.89 us  [on_device(): mine = lax.optimization_barrier(jnp.where(mine == mine, mine, 0.0))]
    add x1, other arithmetic: 2.03 us -> 0.55 us  [on_device(): summed = mine + lax.ppermute(other, 'c', [(0, 1), (1, 0)])]
  transfers between devices with their start and end apart: 2 -> 2, of which waited for: 2 -> 2; matrix products, arithmetic and copies ran while one was open for 1% -> 3% of each run, Pallas kernels for 0% -> 0%
where the time goes in v14:
time: 83.7 us; the launch traced here: 83.5 us
  blocking collectives  61.2 us (73%)
  Pallas kernels  12 us (14%)
  waiting for transfers between devices  4.35 us (5%)
  other arithmetic  3.83 us (5%)
  local copies, waits for them, and re-layouts  2.04 us (2%)
    all_to_all x1, blocking collectives, on_device(): got = lax.all_to_all(summed, ('y', 'xh', 'z', 'xl'), 0, 0, tiled=True)  37.1 us
    all_to_all x1, blocking collectives, gather_blocks(): own = lax.all_to_all(copies, ('y', 'xh'), 0, 0, tiled=True)  24 us
    pallas_call x1, Pallas kernels, add_terms(): pl.pallas_call(sigma_kernel, out_shape=(jax.ShapeDtypeStruct(out_shape, j...  12 us
    ppermute x1, waiting for transfers between devices, on_device(): summed = mine + lax.ppermute(other, 'c', [(0, 1), (1, 0)])  2.34 us
    ppermute x1, waiting for transfers between devices, gather_blocks(): swapped = lax.ppermute(own, 'c', [(0, 1), (1, 0)])  2.01 us
    unnamed x10, local copies, waits for them, and re-layouts  1.96 us
    select_n x1, other arithmetic, on_device(): mine = lax.optimization_barrier(jnp.where(mine == mine, mine, 0.0))  1.89 us
  transfers between devices with their start and end apart: 2, of which 2 were waited for; matrix products, arithmetic and copies ran while one was open for 3% of the time, Pallas kernels for 0%

profile of v14, /device:TPU:0, one launch (start us, length us, event | category | flops | bytes accessed | tf_op | source)
XLA Modules:
  0.0 83.5 jit_solution(13801696237118579121)
XLA Ops:
  0.0 0.0 copy-start
  0.0 0.0 copy-start.3
  0.0 0.0 copy-start.4
  0.0 0.9 %copy-done = bf16[2,256,256]{2,1,0:T(8,128)(2,1)S(1)} copy-done((bf16[2,256,256]{2,1,0:T(8,128)(2,1)S(1)}, bf16[2,256,256]{2,1,0:T(8,128)(2,1)}, u32[]{:S(2)}) %copy-start) | copy-done | bytes 262168
  1.0 0.1 broadcast_in_dim.13
  1.0 24.0 %all_to_all.10.own_ref = bf16[8,256,256]{2,1,0:T(8,128)(2,1)S(1)} all-to-all(bf16[8,256,256]{2,1,0:T(8,128)(2,1)S(1)} %broadcast_in_dim.13), channel_id=1, replica_groups=mesh['y'=4,'xh'=2,'z'=4,'xl'=2,'c'=2] {'y','xh'}, dimensions={0} | all-to-all | bytes 2097152 | tf_op jit(solution)/shard_map/all_to_all | solution.py:71
  25.1 0.0 copy-start.1
  25.1 0.0 collective-permute-start
  25.1 0.0 copy-done.3
  25.1 0.0 copy-done.4
  25.1 0.6 bitcast_add_fusion.src_ref
  25.7 2.0 %collective-permute-done.swapped_ref = bf16[8,256,256]{2,1,0:T(8,128)(2,1)S(1)} collective-permute-done((bf16[8,256,256]{2,1,0:T(8,128)(2,1)S(1)}, bf16[8,256,256]{2,1,0:T(8,128)(2,1)S(1)}, u32[]{:S(2)}, u32[]{:S(2)}) %collective-permute-start) | collective-permute-done | bytes 1048608 | tf_op jit(solution)/shard_map/ppermute | solution.py:72
  27.7 0.0 copy-start.2
  27.7 0.0 copy-done.1
  27.8 1.0 %copy-done.2 = bf16[8,256,256]{2,1,0:T(8,128)(2,1)} copy-done((bf16[8,256,256]{2,1,0:T(8,128)(2,1)}, bf16[8,256,256]{2,1,0:T(8,128)(2,1)S(1)}, u32[]{:S(2)}) %copy-start.2) | copy-done | bytes 1048600
  28.8 12.0 %shard_map.64 = (f32[16,4,32,256]{3,2,1,0:T(8,128)}, f32[16,4,32,256]{3,2,1,0:T(8,128)}) custom-call(s32[1]{0:T(128)} %bitcast.core_ref, s32[64]{0:T(128)} %bitcast_add_fusion.src_ref, s32[64]{0:T(128)} %tgt_ref.1, bf16[8,256,256]{2,1,0:T(8,128)(2,1)} %copy-done.1, bf16[8,256,256]{2,1,0:T(8,128)(2,1)} %copy-done.2, bf16[64,256,256]{2,1,0:T(8,128)(2,1)} %left_ref.1, ...), custom_call_target="tpu_custom_call" | custom-call | tf_op jit(solution)/shard_map/pallas_call | solution.py:53
  40.7 0.1 collective-permute-start.1
  40.8 1.9 %compare_select_fusion = f32[64,32,256]{2,1,0:T(8,128)S(1)} fusion(f32[16,4,32,256]{3,2,1,0:T(8,128)} %get-tuple-element.7), kind=kLoop, calls=%fused_computation | loop fusion | flops 1048576 | bytes 4194304 | tf_op jit(solution)/shard_map/jit(_where)/select_n | solution.py:88
  42.7 2.3 %collective-permute-done.1 = f32[64,32,256]{2,1,0:T(8,128)S(1)} collective-permute-done((f32[64,32,256]{2,1,0:T(8,128)}, f32[64,32,256]{2,1,0:T(8,128)S(1)}, u32[]{:S(2)}, u32[]{:S(2)}) %collective-permute-start.1) | collective-permute-done | bytes 2097184 | tf_op jit(solution)/shard_map/ppermute | solution.py:90
  45.1 0.6 add.12
  45.6 37.1 %all_to_all.11 = f32[64,32,256]{2,1,0:T(8,128)S(1)} all-to-all(f32[64,32,256]{2,1,0:T(8,128)S(1)} %add.12), channel_id=1, replica_groups=mesh['y'=4,'xh'=2,'z'=4,'xl'=2,'c'=2] {'y','xh','z','xl'}, dimensions={0} | all-to-all | bytes 4194304 | tf_op jit(solution)/shard_map/all_to_all | solution.py:91
  82.8 0.8 reduce_sum.9
  (1 shorter events, 0.0 us)
Async XLA Ops:
  0.0 1.0 %copy-start = (bf16[2,256,256]{2,1,0:T(8,128)(2,1)S(1)}, bf16[2,256,256]{2,1,0:T(8,128)(2,1)}, u32[]{:S(2)}) copy-start(bf16[2,256,256]{2,1,0:T(8,128)(2,1)} %param.6) | copy-start | bytes 786436
  0.0 25.1 %copy-start.3 = (s32[64]{0:T(128)S(1)}, s32[64]{0:T(128)}, u32[]{:S(2)}) copy-start(s32[64]{0:T(128)} %param.10) | copy-start | bytes 772
  0.0 25.1 %copy-start.4 = (s32[64,1]{0,1:T(1,128)S(1)}, s32[64,1]{0,1:T(1,128)}, u32[]{:S(2)}) copy-start(s32[64,1]{0,1:T(1,128)} %param.9) | copy-start | bytes 772
  25.1 2.7 %copy-start.1 = (bf16[8,256,256]{2,1,0:T(8,128)(2,1)}, bf16[8,256,256]{2,1,0:T(8,128)(2,1)S(1)}, u32[]{:S(2)}) copy-start(bf16[8,256,256]{2,1,0:T(8,128)(2,1)S(1)} %all_to_all.10.own_ref) | copy-start | bytes 3145732
  25.1 2.7 %collective-permute-start = (bf16[8,256,256]{2,1,0:T(8,128)(2,1)S(1)}, bf16[8,256,256]{2,1,0:T(8,128)(2,1)S(1)}, u32[]{:S(2)}, u32[]{:S(2)}) collective-permute-start(bf16[8,256,256]{2,1,0:T(8,128)(2,1)S(1)} %all_to_all.10.own_ref), channel_id=1, source_target_pairs={{0,1},{1,0},{2,3},{3,2},{4,5},{5,4},{6,7},{7,6},{8,9},{9,8},{10,11... | collective-permute-start | bytes 3145736 | tf_op jit(solution)/shard_map/ppermute | solution.py:72
  27.7 1.0 %copy-start.2 = (bf16[8,256,256]{2,1,0:T(8,128)(2,1)}, bf16[8,256,256]{2,1,0:T(8,128)(2,1)S(1)}, u32[]{:S(2)}) copy-start(bf16[8,256,256]{2,1,0:T(8,128)(2,1)S(1)} %collective-permute-done.swapped_ref) | copy-start | bytes 3145732
  40.7 4.4 %collective-permute-start.1 = (f32[64,32,256]{2,1,0:T(8,128)}, f32[64,32,256]{2,1,0:T(8,128)S(1)}, u32[]{:S(2)}, u32[]{:S(2)}) collective-permute-start(f32[64,32,256]{2,1,0:T(8,128)} %bitcast.8), channel_id=1, source_target_pairs={{0,1},{1,0},{2,3},{3,2},{4,5},{5,4},{6,7},{7,6},{8,9},{9,8},{10,11... | collective-permute-start | bytes 6291464 | tf_op jit(solution)/shard_map/ppermute | solution.py:90

commit v15 on v14

--- a/solution.py
+++ b/solution.py
@@ -66,7 +66,7 @@
 
 def gather_blocks(wavefunction, n_blk):
     core = lax.axis_index("c")
-    mine = lax.dynamic_index_in_dim(wavefunction, core, 0, keepdims=False)
+    mine = jnp.where(core == 0, wavefunction[0], wavefunction[1])
     copies = jnp.broadcast_to(mine[None], (n_blk,) + mine.shape)
     own = lax.all_to_all(copies, ("y", "xh"), 0, 0, tiled=True)
     swapped = lax.ppermute(own, "c", [(0, 1), (1, 0)])

time: 83.7 us -> 83.8 us (level)
  other arithmetic: 3.83 us -> 4.86 us
  local copies, waits for them, and re-layouts: 2.04 us -> 1.09 us
    broadcast_in_dim x0 -> x1, other arithmetic: none -> 1.01 us  [gather_blocks(): copies = jnp.broadcast_to(mine[None], (n_blk,) + mine.shape)]
    unnamed x10 -> x8, local copies, waits for them, and re-layouts: 1.96 us -> 1.02 us
where the time goes in v15:
time: 83.8 us; the launch traced here: 83.6 us
  blocking collectives  61.2 us (73%)
  Pallas kernels  12 us (14%)
  other arithmetic  4.86 us (6%)
  waiting for transfers between devices  4.32 us (5%)
  local copies, waits for them, and re-layouts  1.09 us (1%)
    all_to_all x1, blocking collectives, on_device(): got = lax.all_to_all(summed, ('y', 'xh', 'z', 'xl'), 0, 0, tiled=True)  37.1 us
    all_to_all x1, blocking collectives, gather_blocks(): own = lax.all_to_all(copies, ('y', 'xh'), 0, 0, tiled=True)  24 us
    pallas_call x1, Pallas kernels, add_terms(): pl.pallas_call(sigma_kernel, out_shape=(jax.ShapeDtypeStruct(out_shape, j...  12 us
    ppermute x1, waiting for transfers between devices, on_device(): summed = mine + lax.ppermute(other, 'c', [(0, 1), (1, 0)])  2.33 us
    ppermute x1, waiting for transfers between devices, gather_blocks(): swapped = lax.ppermute(own, 'c', [(0, 1), (1, 0)])  1.98 us
    select_n x1, other arithmetic, on_device(): mine = lax.optimization_barrier(jnp.where(mine == mine, mine, 0.0))  1.89 us
  transfers between devices with their start and end apart: 2, of which 2 were waited for; matrix products, arithmetic and copies ran while one was open for 3% of the time, Pallas kernels for 0%

profile of v15, /device:TPU:0, one launch (start us, length us, event | category | flops | bytes accessed | tf_op | source)
XLA Modules:
  0.0 83.6 jit_solution(2660905377844381896)
XLA Ops:
  0.0 0.0 copy-start.2
  0.0 0.0 copy-start.3
  0.0 1.0 %select_bitcast_fusion = bf16[256,256]{1,0:T(8,128)(2,1)S(1)} fusion(bf16[2,256,256]{2,1,0:T(8,128)(2,1)} %param.6, pred[]{:T(512)S(6)} %eq.6), kind=kLoop, calls=%fused_computation.1 | loop fusion | flops 65536 | bytes 393217 | tf_op jit(solution)/shard_map/broadcast_in_dim | solution.py:70
  1.0 0.1 broadcast_in_dim.13
  1.1 24.0 %all_to_all.10.own_ref = bf16[8,256,256]{2,1,0:T(8,128)(2,1)S(1)} all-to-all(bf16[8,256,256]{2,1,0:T(8,128)(2,1)S(1)} %broadcast_in_dim.13), channel_id=1, replica_groups=mesh['y'=4,'xh'=2,'z'=4,'xl'=2,'c'=2] {'y','xh'}, dimensions={0} | all-to-all | bytes 2097152 | tf_op jit(solution)/shard_map/all_to_all | solution.py:71
  25.1 0.0 copy-start
  25.1 0.0 collective-permute-start
  25.1 0.0 copy-done.2
  25.1 0.0 copy-done.3
  25.2 0.7 bitcast_add_fusion.src_ref
  25.8 2.0 %collective-permute-done.swapped_ref = bf16[8,256,256]{2,1,0:T(8,128)(2,1)S(1)} collective-permute-done((bf16[8,256,256]{2,1,0:T(8,128)(2,1)S(1)}, bf16[8,256,256]{2,1,0:T(8,128)(2,1)S(1)}, u32[]{:S(2)}, u32[]{:S(2)}) %collective-permute-start) | collective-permute-done | bytes 1048608 | tf_op jit(solution)/shard_map/ppermute | solution.py:72
  27.8 0.0 copy-start.1
  27.8 0.0 copy-done
  27.8 1.0 %copy-done.1 = bf16[8,256,256]{2,1,0:T(8,128)(2,1)} copy-done((bf16[8,256,256]{2,1,0:T(8,128)(2,1)}, bf16[8,256,256]{2,1,0:T(8,128)(2,1)S(1)}, u32[]{:S(2)}) %copy-start.1) | copy-done | bytes 1048600
  28.8 12.0 %shard_map.64 = (f32[16,4,32,256]{3,2,1,0:T(8,128)}, f32[16,4,32,256]{3,2,1,0:T(8,128)}) custom-call(s32[1]{0:T(128)} %bitcast.core_ref, s32[64]{0:T(128)} %bitcast_add_fusion.src_ref, s32[64]{0:T(128)} %tgt_ref.1, bf16[8,256,256]{2,1,0:T(8,128)(2,1)} %copy-done, bf16[8,256,256]{2,1,0:T(8,128)(2,1)} %copy-done.1, bf16[64,256,256]{2,1,0:T(8,128)(2,1)} %left_ref.1, ...), custom_call_target="tpu_custom_call" | custom-call | tf_op jit(solution)/shard_map/pallas_call | solution.py:53
  40.8 0.1 collective-permute-start.1
  40.9 1.9 %compare_select_fusion = f32[64,32,256]{2,1,0:T(8,128)S(1)} fusion(f32[16,4,32,256]{3,2,1,0:T(8,128)} %get-tuple-element.7), kind=kLoop, calls=%fused_computation | loop fusion | flops 1048576 | bytes 4194304 | tf_op jit(solution)/shard_map/jit(_where)/select_n | solution.py:88
  42.8 2.3 %collective-permute-done.1 = f32[64,32,256]{2,1,0:T(8,128)S(1)} collective-permute-done((f32[64,32,256]{2,1,0:T(8,128)}, f32[64,32,256]{2,1,0:T(8,128)S(1)}, u32[]{:S(2)}, u32[]{:S(2)}) %collective-permute-start.1) | collective-permute-done | bytes 2097184 | tf_op jit(solution)/shard_map/ppermute | solution.py:90
  45.1 0.6 add.7
  45.7 37.1 %all_to_all.11 = f32[64,32,256]{2,1,0:T(8,128)S(1)} all-to-all(f32[64,32,256]{2,1,0:T(8,128)S(1)} %add.7), channel_id=1, replica_groups=mesh['y'=4,'xh'=2,'z'=4,'xl'=2,'c'=2] {'y','xh','z','xl'}, dimensions={0} | all-to-all | bytes 4194304 | tf_op jit(solution)/shard_map/all_to_all | solution.py:91
  82.8 0.8 reduce_sum.9
Async XLA Ops:
  0.0 25.1 %copy-start.2 = (s32[64]{0:T(128)S(1)}, s32[64]{0:T(128)}, u32[]{:S(2)}) copy-start(s32[64]{0:T(128)} %param.10) | copy-start | bytes 772
  0.0 25.1 %copy-start.3 = (s32[64,1]{0,1:T(1,128)S(1)}, s32[64,1]{0,1:T(1,128)}, u32[]{:S(2)}) copy-start(s32[64,1]{0,1:T(1,128)} %param.9) | copy-start | bytes 772
  25.1 2.7 %copy-start = (bf16[8,256,256]{2,1,0:T(8,128)(2,1)}, bf16[8,256,256]{2,1,0:T(8,128)(2,1)S(1)}, u32[]{:S(2)}) copy-start(bf16[8,256,256]{2,1,0:T(8,128)(2,1)S(1)} %all_to_all.10.own_ref) | copy-start | bytes 3145732
  25.1 2.7 %collective-permute-start = (bf16[8,256,256]{2,1,0:T(8,128)(2,1)S(1)}, bf16[8,256,256]{2,1,0:T(8,128)(2,1)S(1)}, u32[]{:S(2)}, u32[]{:S(2)}) collective-permute-start(bf16[8,256,256]{2,1,0:T(8,128)(2,1)S(1)} %all_to_all.10.own_ref), channel_id=1, source_target_pairs={{0,1},{1,0},{2,3},{3,2},{4,5},{5,4},{6,7},{7,6},{8,9},{9,8},{10,11... | collective-permute-start | bytes 3145736 | tf_op jit(solution)/shard_map/ppermute | solution.py:72
  27.8 1.0 %copy-start.1 = (bf16[8,256,256]{2,1,0:T(8,128)(2,1)}, bf16[8,256,256]{2,1,0:T(8,128)(2,1)S(1)}, u32[]{:S(2)}) copy-start(bf16[8,256,256]{2,1,0:T(8,128)(2,1)S(1)} %collective-permute-done.swapped_ref) | copy-start | bytes 3145732
  40.8 4.4 %collective-permute-start.1 = (f32[64,32,256]{2,1,0:T(8,128)}, f32[64,32,256]{2,1,0:T(8,128)S(1)}, u32[]{:S(2)}, u32[]{:S(2)}) collective-permute-start(f32[64,32,256]{2,1,0:T(8,128)} %bitcast.8), channel_id=1, source_target_pairs={{0,1},{1,0},{2,3},{3,2},{4,5},{5,4},{6,7},{7,6},{8,9},{9,8},{10,11... | collective-permute-start | bytes 6291464 | tf_op jit(solution)/shard_map/ppermute | solution.py:90
